TPU v7x, 256 devices: a whole 4x4x8 slice. The times are simulated.
256 devices in a mesh: fsdp: 16 (over z_hi, x), tensor: 16 (over z_lo, y, core).
Axes of the slice: x: 4, y: 4, z: 8 (z_hi: 4, z_lo: 2; z = z_hi * 2 + z_lo), core: 2. Of those that a mesh axis runs over, the one named last changes fastest.
Arguments:
- tokens: bfloat16 [8192, 3072], P('fsdp'), may hold values from -6 to 6
- weights: bfloat16 [3072, 4, 4096], P('fsdp', None, 'tensor'), may hold values from -0.109375 to 0.109375
- direction: bfloat16 [3072, 4, 4096], P('fsdp', None, 'tensor'), may hold values from -0.109375 to 0.109375
- precision: float32 [3072], replicated, may hold values from 0.25 to 4
Outputs:
- ggn: float32 [3072, 4, 4096], P('fsdp', None, 'tensor')
All inputs are finite; a program needn't handle non-finite values.
Results may differ from a plain program's by a relative error of at most 0.015.
Values may be sent and summed in bfloat16 or wider, within the bound.
No kernel may reach another device: no remote copies, remote signals or barrier semaphores. Data moves between devices by JAX's collectives and lax.ppermute only.
A program may use at most 128 MiB of HBM per device.

v0:
```python
import jax
import jax.numpy as jnp
from jax import lax
from jax.sharding import PartitionSpec as P

HEAD = 128
PATCHES = 256


def layer_norm(rows):
    mean_row = jnp.mean(rows, -1, keepdims=True)
    centred = rows - mean_row
    spread = jnp.mean(centred * centred, -1, keepdims=True)
    return centred * lax.rsqrt(spread + 1e-06)


def attend(queries, key_rows, value_rows):
    query_norm = layer_norm(queries)
    key_norm = layer_norm(key_rows)
    score_scale = queries.shape[-1] ** (-0.5)
    scores = (
        jnp.einsum("bqhe,bkhe->bhqk", query_norm, key_norm, precision=lax.Precision.HIGHEST)
        * score_scale
    )
    exponent = jnp.exp(scores)
    attn_weights = exponent / jnp.sum(exponent, -1, keepdims=True)
    return jnp.einsum("bhqk,bkhe->bqhe", attn_weights, value_rows, precision=lax.Precision.HIGHEST)


def cross_rows(left, right):
    return lax.dot_general(
        left, right, (((1,), (1,)), ((), ())), preferred_element_type=jnp.float32
    )


def over_tokens(left, right):
    return lax.dot_general(
        left, right, (((0,), (0,)), ((), ())), preferred_element_type=jnp.float32
    )


def body(tokens, weights, direction, precision):
    model_width = tokens.shape[1]
    local_rows = tokens.shape[0]
    head_cols = weights.shape[2]
    normed = layer_norm(tokens.astype(jnp.float32)).astype(jnp.bfloat16)
    full_weights = lax.all_gather(weights, "fsdp", axis=0, tiled=True)
    full_direction = lax.all_gather(direction, "fsdp", axis=0, tiled=True)
    in_weights = full_weights[:, 0:3, :].reshape(model_width, 3 * head_cols)
    in_direction = full_direction[:, 0:3, :].reshape(model_width, 3 * head_cols)
    projected = jnp.dot(normed, in_weights, preferred_element_type=jnp.float32).astype(jnp.bfloat16)
    tangent_in = jnp.dot(normed, in_direction, preferred_element_type=jnp.float32).astype(
        jnp.bfloat16
    )

    def to_heads(block):
        return block.astype(jnp.float32).reshape(
            local_rows // PATCHES, PATCHES, 3, head_cols // HEAD, HEAD
        )

    primal = to_heads(projected)
    tangent_heads = to_heads(tangent_in)
    primal_args = (primal[:, :, 0], primal[:, :, 1], primal[:, :, 2])
    tangent_args = (tangent_heads[:, :, 0], tangent_heads[:, :, 1], tangent_heads[:, :, 2])
    mixed, mixed_dot = jax.jvp(attend, primal_args, tangent_args)
    mixed_rows = mixed.reshape(local_rows, head_cols).astype(jnp.bfloat16)
    tangent_out = mixed_dot.reshape(local_rows, head_cols).astype(jnp.bfloat16)
    out_weights = full_weights[:, 3, :]
    out_direction = full_direction[:, 3, :]
    partial_sum = cross_rows(tangent_out, out_weights) + cross_rows(mixed_rows, out_direction)
    output_dot = lax.psum(partial_sum.astype(jnp.bfloat16), "tensor").astype(jnp.float32)
    cotangent = (precision * output_dot).astype(jnp.bfloat16)
    share_rows = model_width // lax.axis_size("fsdp")
    back_rows = jnp.dot(cotangent, out_weights, preferred_element_type=jnp.float32)
    back_rows = back_rows.reshape(local_rows // PATCHES, PATCHES, head_cols // HEAD, HEAD)
    primal_out, pullback = jax.vjp(attend, *primal_args)
    gradients = pullback(back_rows)
    stacked = jnp.stack(gradients, axis=2).reshape(local_rows, 3 * head_cols).astype(jnp.bfloat16)
    return lax.psum_scatter(
        jnp.concatenate(
            [
                over_tokens(normed, stacked).reshape(
                    lax.axis_size("fsdp") * share_rows, 3, head_cols
                ),
                over_tokens(cotangent, mixed_rows)[:, None, :],
            ],
            axis=1,
        ).astype(jnp.bfloat16),
        "fsdp",
        scatter_dimension=0,
        tiled=True,
    ).astype(jnp.float32)


def solution(mesh):
    return jax.shard_map(
        body,
        mesh=mesh,
        in_specs=(P("fsdp", None), P("fsdp", None, "tensor"), P("fsdp", None, "tensor"), P()),
        out_specs=P("fsdp", None, "tensor"),
        check_vma=False,
    )
```

profile of v0, /device:TPU:8, one launch (start us, length us, event | category | flops | bytes accessed | tf_op | source)
XLA Modules:
  0.0 533.3 jit_solution(97903180383077813)
XLA Ops:
  6.5 0.7 all-gather.5.cloned.1.call-update
  7.3 0.7 all-gather.3.cloned.1.call-update
  8.1 2.4 convert_reduce_fusion
  10.4 1.0 fusion.2
  11.4 91.5 %all-gather.5.cloned.1.call-done = bf16[3072,4,256]{2,1,0:T(4,128)(2,1)} async-done(((bf16[192,4,256]{2,1,0:T(4,128)(2,1)}), bf16[3072,4,256]{2,1,0:T(4,128)(2,1)}) %all-gather.5.cloned.1.call-update) | async-done | bytes 6291472 | tf_op jit(solution)/shard_map/all_gather | solution.py:47
  102.9 10.1 %copy.106 = bf16[3072,3,256]{0,2,1:T(8,128)(2,1)} copy(bf16[3072,3,256]{2,1,0:T(4,128)(2,1)} %bitcast.153) | data formatting | bytes 9437184
  113.0 5.9 %convolution_convert_fusion.2 = bf16[512,768]{1,0:T(8,128)(2,1)} fusion(bf16[3072,768]{0,1:T(8,128)(2,1)} %bitcast.157, bf16[512,3072]{1,0:T(8,128)(2,1)S(1)} %copy-done.1, f32[512]{0:T(512)S(1)} %add_rsqrt_fusion, f32[512]{0:T(512)S(1)} %broadcast_multiply_fusion.4), kind=kOutput, calls=%fused_computation.16 | convolution fusion | flops 2422603776 | bytes 8654848 | tf_op jit(solution)/shard_map/dot_general | solution.py:51
  118.9 2.0 reshape.137
  120.9 1.0 copy.60
  122.2 78.6 %all-gather.3.cloned.1.call-done = bf16[3072,4,256]{2,1,0:T(4,128)(2,1)} async-done(((bf16[192,4,256]{2,1,0:T(4,128)(2,1)}), bf16[3072,4,256]{2,1,0:T(4,128)(2,1)}) %all-gather.3.cloned.1.call-update) | async-done | bytes 6291472 | tf_op jit(solution)/shard_map/all_gather | solution.py:48
  200.8 10.1 %copy.105 = bf16[3072,3,256]{0,2,1:T(8,128)(2,1)} copy(bf16[3072,3,256]{2,1,0:T(4,128)(2,1)} %bitcast.154) | data formatting | bytes 9437184
  210.9 5.9 %convolution_convert_fusion.3 = bf16[512,768]{1,0:T(8,128)(2,1)S(1)} fusion(bf16[3072,768]{0,1:T(8,128)(2,1)} %bitcast.158, bf16[512,3072]{1,0:T(8,128)(2,1)} %param.4, f32[512]{0:T(512)S(1)} %add_rsqrt_fusion, f32[512]{0:T(512)S(1)} %broadcast_multiply_fusion.4), kind=kOutput, calls=%fused_computation.17 | convolution fusion | flops 2422603776 | bytes 8654848 | tf_op jit(solution)/shard_map/dot_general | solution.py:52
  216.9 0.2 reshape.135
  217.0 2.1 copy.58
  219.1 1.3 reshape.139
  220.5 0.3 multiply_reduce_fusion.1
  220.9 1.2 fusion.65
  222.0 2.4 fusion.11
  224.4 2.3 fusion.42
  226.7 1.1 copy.74
  227.9 1.1 fusion.23
  229.1 1.3 fusion.66
  230.4 1.6 fusion.13
  232.2 6.2 %slice.48 = bf16[3072,1,256]{2,1,0:T(2,128)(2,1)S(1)} slice(bf16[3072,4,256]{2,1,0:T(4,128)(2,1)} %all-gather.5.cloned.1.call-done), slice={[0:3072], [3:4], [0:256]} | slice | bytes 3145728 | tf_op jit(solution)/shard_map/slice | solution.py:68
  238.5 1.0 fusion.6
  239.5 0.7 copy-done
  240.1 1.0 slice-done.1
  241.2 3.4 slice.49
  244.6 2.7 add_convert_fusion
  247.4 6.4 %copy.109 = bf16[3072,1,256]{0,2,1:T(8,128)(2,1)S(1)} copy(bf16[3072,1,256]{2,1,0:T(2,128)(2,1)} %copy-done) | data formatting | bytes 3145728 | tf_op jit(solution)/shard_map/dot_general | solution.py:74
  253.9 126.4 %all-reduce.2.cloned.1.call-done = bf16[512,3072]{1,0:T(8,128)(2,1)} async-done(((bf16[512,3072]{1,0:T(8,128)(2,1)}), bf16[512,3072]{1,0:T(8,128)(2,1)}) %all-reduce.2.cloned.1.call-update) | async-done | bytes 3145744 | tf_op jit(solution)/shard_map/psum | solution.py:71
  380.2 2.6 multiply_convert_fusion
  382.8 1.0 convolution_bitcast_fusion.2
  383.9 0.2 copy-done.5
  384.1 1.6 multiply_reduce_fusion
  385.7 1.3 fusion.12
  387.0 2.2 fusion.4
  389.2 1.0 multiply_reduce_fusion.4
  390.2 1.5 fusion.58
  391.9 0.3 fusion.36
  392.2 1.0 pad_maximum_fusion.1
  393.2 3.3 copy.83
  396.4 3.1 convert_element_type.64
  399.6 2.3 copy.84
  401.9 4.8 convolution_convert_fusion
  406.7 3.2 pad_maximum_fusion
  409.9 114.6 %reduce-scatter.2.cloned.1.call-done = bf16[192,4,256]{2,0,1:T(8,128)(2,1)} async-done(((bf16[3072,4,256]{2,0,1:T(8,128)(2,1)}), bf16[192,4,256]{2,0,1:T(8,128)(2,1)}) %reduce-scatter.2.cloned.1.call-update) | async-done | bytes 393232 | tf_op jit(solution)/shard_map/reduce_scatter | solution.py:79
  524.5 2.2 copy.86
  (46 shorter events, 1.0 us)
Async XLA Ops:
  6.5 3.9 copy-start.1
  6.5 96.4 %all-gather.5.cloned.1.call-start = ((), (), s32[]{:S(2)}) async-start(), calls=%async_computation.2 | async-start | bytes 6684672 | tf_op jit(solution)/shard_map/all_gather | solution.py:47
  7.3 193.5 %all-gather.3.cloned.1.call-start = ((), (), s32[]{:S(2)}) async-start(), calls=%async_computation.1 | async-start | bytes 6684672 | tf_op jit(solution)/shard_map/all_gather | solution.py:48
  8.0 372.2 %all-reduce.2.cloned.1.call-start = ((), (), s32[]{:S(2)}) async-start(), calls=%async_computation.3 | async-start | bytes 6291456 | tf_op jit(solution)/shard_map/psum | solution.py:71
  121.9 89.0 %copy-start.6 = (bf16[2,256,3,2,128]{1,4,3,0,2:T(8,128)(2,1)}, bf16[2,256,3,2,128]{1,4,3,0,2:T(8,128)(2,1)S(1)}, u32[]{:S(2)}) copy-start(bf16[2,256,3,2,128]{1,4,3,0,2:T(8,128)(2,1)S(1)} %copy.60) | copy-start | bytes 2359300
  222.0 4.7 copy-start.3
  227.9 1.2 copy-start.4
  227.9 2.5 copy-start.9
  232.2 8.0 %slice-start = ((s8[6291456]{0:T(1024)(128)(4,1)}), s8[4194304]{0:T(1024)(128)(4,1)S(1)}, s32[]{:S(2)}) async-start(s8[6291456]{0:T(1024)(128)(4,1)} %bitcast.155), calls=%async_computation.5 | async-start | bytes 8388608
  238.4 1.7 copy-start
  238.4 2.7 slice-start.1
  247.4 132.9 %copy-start.8 = (f32[3072]{0:T(1024)S(1)}, f32[3072]{0:T(1024)}, u32[]{:S(2)}) copy-start(f32[3072]{0:T(1024)} %param.7) | copy-start | bytes 36868
  247.4 277.2 %reduce-scatter.2.cloned.1.call-start = ((), (), s32[]{:S(2)}) async-start(), calls=%async_computation.4 | async-start | bytes 6684672 | tf_op jit(solution)/shard_map/reduce_scatter | solution.py:79
  382.8 1.2 copy-start.5
  392.2 9.7 %copy-start.2 = (bf16[512,3072]{1,0:T(8,128)(2,1)S(1)}, bf16[512,3072]{1,0:T(8,128)(2,1)}, u32[]{:S(2)}) copy-start(bf16[512,3072]{1,0:T(8,128)(2,1)} %param.4) | copy-start | bytes 9437188
  401.9 4.8 copy-start.7
Sparse Core Ops, SparseCore 0:
  9.8 93.0 all-gather.4
  105.3 95.4 all-gather.2
  247.5 132.7 all-reduce.1
  410.0 114.4 reduce-scatter.1
where the time goes:
time: 535 us; the launch traced here: 533 us
  waiting for transfers between devices  412 us (77%)
  local copies, waits for them, and re-layouts  55.8 us (10%)
  matrix products  38.9 us (7%)
  between operations  13.5 us (3%)
  other arithmetic  12.5 us (2%)
    psum x1, waiting for transfers between devices, body(): lax.psum(partial_sum.astype(jnp.bfloat16), 'tensor').astype(jnp.float32)  126 us
    reduce_scatter x1, waiting for transfers between devices, body(): lax.psum_scatter(jnp.concatenate([over_tokens(normed, stacked).reshape(la...  115 us
    all_gather x1, waiting for transfers between devices, body(): full_weights = lax.all_gather(weights, 'fsdp', axis=0, tiled=True)  91.5 us
    all_gather x1, waiting for transfers between devices, body(): full_direction = lax.all_gather(direction, 'fsdp', axis=0, tiled=True)  78.6 us
    unnamed x26, local copies, waits for them, and re-layouts  22.2 us
  transfers between devices with their start and end apart: 4, of which 4 were waited for; matrix products, arithmetic and copies ran while one was open for 5% of the time, Pallas kernels for 0%

commit v1 on v0

--- a/solution.py
+++ b/solution.py
@@ -44,8 +44,9 @@
     local_rows = tokens.shape[0]
     head_cols = weights.shape[2]
     normed = layer_norm(tokens.astype(jnp.float32)).astype(jnp.bfloat16)
-    full_weights = lax.all_gather(weights, "fsdp", axis=0, tiled=True)
-    full_direction = lax.all_gather(direction, "fsdp", axis=0, tiled=True)
+    both = lax.all_gather(jnp.concatenate([weights, direction], 1), "fsdp", axis=0, tiled=True)
+    full_weights = both[:, 0:4]
+    full_direction = both[:, 4:8]
     in_weights = full_weights[:, 0:3, :].reshape(model_width, 3 * head_cols)
     in_direction = full_direction[:, 0:3, :].reshape(model_width, 3 * head_cols)
     projected = jnp.dot(normed, in_weights, preferred_element_type=jnp.float32).astype(jnp.bfloat16)
@@ -68,8 +69,18 @@
     out_weights = full_weights[:, 3, :]
     out_direction = full_direction[:, 3, :]
     partial_sum = cross_rows(tangent_out, out_weights) + cross_rows(mixed_rows, out_direction)
-    output_dot = lax.psum(partial_sum.astype(jnp.bfloat16), "tensor").astype(jnp.float32)
-    cotangent = (precision * output_dot).astype(jnp.bfloat16)
+    n_tensor = lax.axis_size("tensor")
+    chunk = model_width // n_tensor
+    arrived = lax.all_to_all(
+        partial_sum.astype(jnp.bfloat16).reshape(local_rows, n_tensor, chunk), "tensor", 1, 1
+    )
+    output_dot = jnp.sum(arrived.astype(jnp.float32), 1)
+    own_precision = lax.dynamic_slice_in_dim(precision, lax.axis_index("tensor") * chunk, chunk)
+    cotangent_part = (own_precision * output_dot).astype(jnp.bfloat16)
+    spread = jnp.broadcast_to(cotangent_part[None], (n_tensor, local_rows, chunk))
+    cotangent = jnp.moveaxis(lax.all_to_all(spread, "tensor", 0, 0), 0, 1).reshape(
+        local_rows, model_width
+    )
     share_rows = model_width // lax.axis_size("fsdp")
     back_rows = jnp.dot(cotangent, out_weights, preferred_element_type=jnp.float32)
     back_rows = back_rows.reshape(local_rows // PATCHES, PATCHES, head_cols // HEAD, HEAD)

time: 535 us -> 521 us (0.974)
  waiting for transfers between devices: 412 us -> 338 us
  local copies, waits for them, and re-layouts: 55.8 us -> 87.7 us
  starting transfers between devices: 0.12 us -> 23.1 us
    psum x1 -> x0, waiting for transfers between devices: 126 us -> none  [body(): lax.psum(partial_sum.astype(jnp.bfloat16), 'tensor').astype(jnp.float32)]
    all_to_all x0 -> x2, waiting for transfers between devices: none -> 80.4 us  [the longest x1 43.1 us: body(): lax.all_to_all(partial_sum.astype(jnp.bfloat16).reshape(local_rows, n_ten...]
    all_to_all x0 -> x2, starting transfers between devices: none -> 23.1 us  [the longest x1 16.2 us: body(): lax.all_to_all(partial_sum.astype(jnp.bfloat16).reshape(local_rows, n_ten...]
    all_gather x2 -> x1, waiting for transfers between devices: 170 us -> 149 us  [body(): lax.all_gather(jnp.concatenate([weights, direction], 1), 'fsdp', axis=0,...]
    slice x1, local copies, waits for them, and re-layouts: 3.4 us -> 13.8 us  [body(): out_direction = full_direction[:, 3, :]]
    slice x1, local copies, waits for them, and re-layouts: 6.25 us -> 15.9 us  [body(): in_weights = full_weights[:, 0:3, :].reshape(model_width, 3 * head_cols)]
    dot_general x1 -> x2, local copies, waits for them, and re-layouts: 6.44 us -> 11.9 us  [body(): jnp.dot(cotangent, out_weights, preferred_element_type=jnp.float32)]
    reduce_scatter x1, waiting for transfers between devices: 115 us -> 109 us  [body(): lax.psum_scatter(jnp.concatenate([over_tokens(normed, stacked).reshape(la...]
  transfers between devices with their start and end apart: 4 -> 4, of which waited for: 4 -> 4; matrix products, arithmetic and copies ran while one was open for 5% -> 2% of each run, Pallas kernels for 0% -> 0%
where the time goes in v1:
time: 521 us; the launch traced here: 519 us
  waiting for transfers between devices  338 us (65%)
  local copies, waits for them, and re-layouts  87.7 us (17%)
  matrix products  41.4 us (8%)
  starting transfers between devices  23.1 us (4%)
  other arithmetic  14.9 us (3%)
  between operations  13.7 us (3%)
    all_gather x1, waiting for transfers between devices, body(): lax.all_gather(jnp.concatenate([weights, direction], 1), 'fsdp', axis=0,...  149 us
    reduce_scatter x1, waiting for transfers between devices, body(): lax.psum_scatter(jnp.concatenate([over_tokens(normed, stacked).reshape(la...  109 us
    all_to_all x1, waiting for transfers between devices, body(): lax.all_to_all(partial_sum.astype(jnp.bfloat16).reshape(local_rows, n_ten...  43.1 us
    all_to_all x1, waiting for transfers between devices, body(): lax.all_to_all(spread, 'tensor', 0, 0)  37.3 us
    unnamed x18, local copies, waits for them, and re-layouts  21.1 us
    all_to_all x1, starting transfers between devices, body(): lax.all_to_all(partial_sum.astype(jnp.bfloat16).reshape(local_rows, n_ten...  16.2 us
    slice x1, local copies, waits for them, and re-layouts, body(): in_weights = full_weights[:, 0:3, :].reshape(model_width, 3 * head_cols)  15.9 us
    slice x1, local copies, waits for them, and re-layouts, body(): out_direction = full_direction[:, 3, :]  13.8 us
  transfers between devices with their start and end apart: 4, of which 4 were waited for; matrix products, arithmetic and copies ran while one was open for 2% of the time, Pallas kernels for 0%

profile of v1, /device:TPU:8, one launch (start us, length us, event | category | flops | bytes accessed | tf_op | source)
XLA Modules:
  0.0 519.1 jit_solution(14483191044745188765)
XLA Ops:
  6.5 2.5 pad_maximum_fusion.1
  9.1 2.4 convert_reduce_fusion
  11.5 1.0 fusion.2
  12.5 148.7 %all-gather.2.cloned.1.call-done = bf16[3072,8,256]{2,1,0:T(8,128)(2,1)} async-done(((bf16[192,8,256]{2,1,0:T(8,128)(2,1)}), bf16[3072,8,256]{2,1,0:T(8,128)(2,1)}) %all-gather.2.cloned.1.call-update) | async-done | bytes 12582928 | tf_op jit(solution)/shard_map/all_gather | solution.py:47
  161.1 15.9 %fusion.71 = (bf16[3072,3,256]{2,1,0:T(4,128)(2,1)}, bf16[3072,3,256]{2,1,0:T(4,128)(2,1)}) fusion(bf16[3072,8,256]{2,1,0:T(8,128)(2,1)} %all-gather.2.cloned.1.call-done), kind=kLoop, calls=%fused_computation.127 | loop fusion | bytes 18874368 | tf_op jit(solution)/shard_map/slice | solution.py:50
  177.0 10.2 %copy.112 = bf16[3072,3,256]{0,2,1:T(8,128)(2,1)} copy(bf16[3072,3,256]{2,1,0:T(4,128)(2,1)} %get-tuple-element.21) | data formatting | bytes 9437184
  187.2 5.9 %convolution_convert_fusion.2 = bf16[512,768]{1,0:T(8,128)(2,1)} fusion(bf16[3072,768]{0,1:T(8,128)(2,1)} %bitcast.153, bf16[512,3072]{1,0:T(8,128)(2,1)S(1)} %copy-done.1, f32[512]{0:T(512)S(1)} %add_rsqrt_fusion, f32[512]{0:T(512)S(1)} %broadcast_multiply_fusion.4), kind=kOutput, calls=%fused_computation.18 | convolution fusion | flops 2422603776 | bytes 8654848 | tf_op jit(solution)/shard_map/dot_general | solution.py:52
  193.1 2.0 reshape.162
  195.1 1.0 copy.62
  196.4 10.2 %copy.111 = bf16[3072,3,256]{0,2,1:T(8,128)(2,1)} copy(bf16[3072,3,256]{2,1,0:T(4,128)(2,1)} %get-tuple-element.22) | data formatting | bytes 9437184
  206.6 5.9 %convolution_convert_fusion.3 = bf16[512,768]{1,0:T(8,128)(2,1)S(1)} fusion(bf16[3072,768]{0,1:T(8,128)(2,1)} %bitcast.154, bf16[512,3072]{1,0:T(8,128)(2,1)} %param.4, f32[512]{0:T(512)S(1)} %add_rsqrt_fusion, f32[512]{0:T(512)S(1)} %broadcast_multiply_fusion.4), kind=kOutput, calls=%fused_computation.19 | convolution fusion | flops 2422603776 | bytes 8654848 | tf_op jit(solution)/shard_map/dot_general | solution.py:53
  212.7 2.1 copy.60
  214.8 1.3 reshape.164
  216.6 1.2 fusion.72
  217.7 2.4 fusion.16
  220.1 2.3 fusion.47
  222.4 1.1 copy.76
  223.6 1.1 fusion.28
  224.8 1.3 fusion.73
  226.1 1.6 fusion.18
  227.9 13.8 %fusion.70 = (bf16[3072,1,256]{2,1,0:T(2,128)(2,1)S(1)}, bf16[3072,1,256]{2,1,0:T(2,128)(2,1)S(1)}) fusion(bf16[3072,8,256]{2,1,0:T(8,128)(2,1)} %all-gather.2.cloned.1.call-done), kind=kLoop, calls=%fused_computation.126 | loop fusion | bytes 6291456 | tf_op jit(solution)/shard_map/slice | solution.py:70
  241.7 1.0 fusion.8
  242.7 0.7 copy-done
  243.4 2.7 add_convert_fusion
  246.1 4.7 copy.78
  250.8 16.2 %all-to-all-start = ((bf16[512,16,192]{0,2,1:T(8,128)(2,1)}), bf16[512,16,192]{0,2,1:T(8,128)(2,1)}, u32[]{:S(2)}, u32[]{:S(2)}) async-start(bf16[512,16,192]{0,2,1:T(8,128)(2,1)} %bitcast.152), calls=%async_computation | async-start | bytes 6291456 | tf_op jit(solution)/shard_map/all_to_all | solution.py:74
  266.9 0.8 dynamic_slice.3
  267.7 43.1 %all-to-all-done = bf16[512,16,192]{0,2,1:T(8,128)(2,1)} async-done(((bf16[512,16,192]{0,2,1:T(8,128)(2,1)}), bf16[512,16,192]{0,2,1:T(8,128)(2,1)}, u32[]{:S(2)}, u32[]{:S(2)}) %all-to-all-start) | async-done | bytes 3145760 | tf_op jit(solution)/shard_map/all_to_all | solution.py:74
  310.8 2.4 convert_reduce_fusion.1
  313.3 2.0 broadcast_in_dim.15
  315.3 6.9 %all-to-all-start.1 = ((bf16[16,512,192]{1,2,0:T(8,128)(2,1)}), bf16[16,512,192]{1,2,0:T(8,128)(2,1)}, u32[]{:S(2)}, u32[]{:S(2)}) async-start(bf16[16,512,192]{1,2,0:T(8,128)(2,1)} %broadcast_in_dim.15), calls=%async_computation.1 | async-start | bytes 6291456 | tf_op jit(solution)/shard_map/all_to_all | solution.py:81
  322.2 6.4 %copy.115 = bf16[3072,1,256]{0,2,1:T(8,128)(2,1)S(1)} copy(bf16[3072,1,256]{2,1,0:T(2,128)(2,1)} %copy-done) | data formatting | bytes 3145728 | tf_op jit(solution)/shard_map/dot_general | solution.py:85
  328.6 37.3 %all-to-all-done.1 = bf16[16,512,192]{1,2,0:T(8,128)(2,1)} async-done(((bf16[16,512,192]{1,2,0:T(8,128)(2,1)}), bf16[16,512,192]{1,2,0:T(8,128)(2,1)}, u32[]{:S(2)}, u32[]{:S(2)}) %all-to-all-start.1) | async-done | bytes 3145760 | tf_op jit(solution)/shard_map/all_to_all | solution.py:81
  366.0 5.5 %dot_general.72 = bf16[2,256,3072]{1,0,2:T(2,128)(2,1)} reshape(bf16[512,16,192]{0,2,1:T(8,128)(2,1)} %bitcast.14) | data formatting | bytes 6291456 | tf_op jit(solution)/shard_map/dot_general | solution.py:85
  371.5 3.0 fusion.12
  374.5 1.7 multiply_reduce_fusion
  376.1 1.3 fusion.17
  377.5 1.0 multiply_reduce_fusion.4
  378.5 1.5 fusion.63
  380.4 1.0 pad_maximum_fusion.2
  381.4 3.3 copy.87
  384.7 3.1 convert_element_type.67
  387.8 2.3 copy.88
  390.1 4.7 convolution_convert_fusion
  394.8 2.9 fusion.4
  397.7 3.2 pad_maximum_fusion
  400.9 109.2 %reduce-scatter.2.cloned.1.call-done = bf16[192,4,256]{2,0,1:T(8,128)(2,1)} async-done(((bf16[3072,4,256]{2,0,1:T(8,128)(2,1)}), bf16[192,4,256]{2,0,1:T(8,128)(2,1)}) %reduce-scatter.2.cloned.1.call-update) | async-done | bytes 393232 | tf_op jit(solution)/shard_map/reduce_scatter | solution.py:90
  510.1 2.2 copy.90
  (41 shorter events, 1.7 us)
Async XLA Ops:
  6.5 4.9 copy-start.1
  6.5 154.6 %all-gather.2.cloned.1.call-start = ((), (), s32[]{:S(2)}) async-start(), calls=%async_computation.3 | async-start | bytes 13369344 | tf_op jit(solution)/shard_map/all_gather | solution.py:47
  196.1 10.5 %copy-start.6 = (bf16[2,256,3,2,128]{1,4,3,0,2:T(8,128)(2,1)}, bf16[2,256,3,2,128]{1,4,3,0,2:T(8,128)(2,1)S(1)}, u32[]{:S(2)}) copy-start(bf16[2,256,3,2,128]{1,4,3,0,2:T(8,128)(2,1)S(1)} %copy.62) | copy-start | bytes 2359300
  217.7 4.7 copy-start.3
  223.6 1.2 copy-start.4
  223.6 2.5 copy-start.7
  241.7 1.7 copy-start
  250.8 60.0 %all-to-all-start = ((bf16[512,16,192]{0,2,1:T(8,128)(2,1)}), bf16[512,16,192]{0,2,1:T(8,128)(2,1)}, u32[]{:S(2)}, u32[]{:S(2)}) async-start(bf16[512,16,192]{0,2,1:T(8,128)(2,1)} %bitcast.152), calls=%async_computation | async-start | bytes 6291456 | tf_op jit(solution)/shard_map/all_to_all | solution.py:74
  315.3 50.7 %all-to-all-start.1 = ((bf16[16,512,192]{1,2,0:T(8,128)(2,1)}), bf16[16,512,192]{1,2,0:T(8,128)(2,1)}, u32[]{:S(2)}, u32[]{:S(2)}) async-start(bf16[16,512,192]{1,2,0:T(8,128)(2,1)} %broadcast_in_dim.15), calls=%async_computation.1 | async-start | bytes 6291456 | tf_op jit(solution)/shard_map/all_to_all | solution.py:81
  322.1 188.0 %reduce-scatter.2.cloned.1.call-start = ((), (), s32[]{:S(2)}) async-start(), calls=%async_computation.4 | async-start | bytes 6684672 | tf_op jit(solution)/shard_map/reduce_scatter | solution.py:90
  371.5 3.0 copy-start.5
  380.4 9.7 %copy-start.2 = (bf16[512,3072]{1,0:T(8,128)(2,1)S(1)}, bf16[512,3072]{1,0:T(8,128)(2,1)}, u32[]{:S(2)}) copy-start(bf16[512,3072]{1,0:T(8,128)(2,1)} %param.4) | copy-start | bytes 9437188
Sparse Core Ops, SparseCore 0:
  9.8 151.3 all-gather.1
  401.0 109.0 reduce-scatter.1

commit v2 on v1

--- a/solution.py
+++ b/solution.py
@@ -42,17 +42,18 @@
 def body(tokens, weights, direction, precision):
     model_width = tokens.shape[1]
     local_rows = tokens.shape[0]
+    share_rows = weights.shape[0]
     head_cols = weights.shape[2]
     normed = layer_norm(tokens.astype(jnp.float32)).astype(jnp.bfloat16)
-    both = lax.all_gather(jnp.concatenate([weights, direction], 1), "fsdp", axis=0, tiled=True)
-    full_weights = both[:, 0:4]
-    full_direction = both[:, 4:8]
-    in_weights = full_weights[:, 0:3, :].reshape(model_width, 3 * head_cols)
-    in_direction = full_direction[:, 0:3, :].reshape(model_width, 3 * head_cols)
-    projected = jnp.dot(normed, in_weights, preferred_element_type=jnp.float32).astype(jnp.bfloat16)
-    tangent_in = jnp.dot(normed, in_direction, preferred_element_type=jnp.float32).astype(
-        jnp.bfloat16
-    )
+    local = jnp.concatenate(
+        [weights[:, 0:3], direction[:, 0:3], weights[:, 3:4], direction[:, 3:4]], 1
+    ).reshape(share_rows, 8 * head_cols)
+    gathered = lax.all_gather(local.T, "fsdp", axis=1, tiled=True)
+    in_both = gathered[: 6 * head_cols]
+    out_both = gathered[6 * head_cols :]
+    both_in = cross_rows(normed, in_both).astype(jnp.bfloat16)
+    projected = both_in[:, : 3 * head_cols]
+    tangent_in = both_in[:, 3 * head_cols :]
 
     def to_heads(block):
         return block.astype(jnp.float32).reshape(
@@ -66,9 +67,12 @@
     mixed, mixed_dot = jax.jvp(attend, primal_args, tangent_args)
     mixed_rows = mixed.reshape(local_rows, head_cols).astype(jnp.bfloat16)
     tangent_out = mixed_dot.reshape(local_rows, head_cols).astype(jnp.bfloat16)
-    out_weights = full_weights[:, 3, :]
-    out_direction = full_direction[:, 3, :]
-    partial_sum = cross_rows(tangent_out, out_weights) + cross_rows(mixed_rows, out_direction)
+    partial_sum = lax.dot_general(
+        jnp.concatenate([tangent_out, mixed_rows], 1),
+        out_both,
+        (((1,), (0,)), ((), ())),
+        preferred_element_type=jnp.float32,
+    )
     n_tensor = lax.axis_size("tensor")
     chunk = model_width // n_tensor
     arrived = lax.all_to_all(
@@ -81,8 +85,7 @@
     cotangent = jnp.moveaxis(lax.all_to_all(spread, "tensor", 0, 0), 0, 1).reshape(
         local_rows, model_width
     )
-    share_rows = model_width // lax.axis_size("fsdp")
-    back_rows = jnp.dot(cotangent, out_weights, preferred_element_type=jnp.float32)
+    back_rows = cross_rows(cotangent, out_both[:head_cols])
     back_rows = back_rows.reshape(local_rows // PATCHES, PATCHES, head_cols // HEAD, HEAD)
     primal_out, pullback = jax.vjp(attend, *primal_args)
     gradients = pullback(back_rows)
@@ -90,9 +93,7 @@
     return lax.psum_scatter(
         jnp.concatenate(
             [
-                over_tokens(normed, stacked).reshape(
-                    lax.axis_size("fsdp") * share_rows, 3, head_cols
-                ),
+                over_tokens(normed, stacked).reshape(model_width, 3, head_cols),
                 over_tokens(cotangent, mixed_rows)[:, None, :],
             ],
             axis=1,

time: 521 us -> 470 us (0.902)
  local copies, waits for them, and re-layouts: 87.7 us -> 41.7 us
    slice x2 -> x5, local copies, waits for them, and re-layouts: 29.7 us -> 7.93 us  [the longest x2 5.25 us: body(): back_rows = cross_rows(cotangent, out_both[:head_cols])]
    unnamed x18 -> x13, local copies, waits for them, and re-layouts: 21.1 us -> 3.78 us
    dot_general x3 -> x1, matrix products: 14.8 us -> 5.49 us  [body(): lax.dot_general(jnp.concatenate([tangent_out, mixed_rows], 1), out_both,...]
    dot_general x2, matrix products: 3.77 us -> 11.1 us  [cross_rows(): lax.dot_general(left, right, (((1,), (1,)), ((), ())), preferred_element_...]
    dot_general x2 -> x1, local copies, waits for them, and re-layouts: 11.9 us -> 5.53 us  [cross_rows(): lax.dot_general(left, right, (((1,), (1,)), ((), ())), preferred_element_...]
where the time goes in v2:
time: 470 us; the launch traced here: 469 us
  waiting for transfers between devices  341 us (73%)
  local copies, waits for them, and re-layouts  41.7 us (9%)
  matrix products  37.6 us (8%)
  starting transfers between devices  23.1 us (5%)
  between operations  13.7 us (3%)
  other arithmetic  11.4 us (2%)
    all_gather x1, waiting for transfers between devices, body(): gathered = lax.all_gather(local.T, 'fsdp', axis=1, tiled=True)  150 us
    reduce_scatter x1, waiting for transfers between devices, body(): lax.psum_scatter(jnp.concatenate([over_tokens(normed, stacked).reshape(mo...  110 us
    all_to_all x1, waiting for transfers between devices, body(): lax.all_to_all(partial_sum.astype(jnp.bfloat16).reshape(local_rows, n_ten...  43.1 us
    all_to_all x1, waiting for transfers between devices, body(): lax.all_to_all(spread, 'tensor', 0, 0)  38.5 us
    all_to_all x1, starting transfers between devices, body(): lax.all_to_all(partial_sum.astype(jnp.bfloat16).reshape(local_rows, n_ten...  16.2 us
    dot_general x2, matrix products, cross_rows(): lax.dot_general(left, right, (((1,), (1,)), ((), ())), preferred_element_...  11.1 us
  transfers between devices with their start and end apart: 4, of which 4 were waited for; matrix products, arithmetic and copies ran while one was open for 2% of the time, Pallas kernels for 0%

profile of v2, /device:TPU:8, one launch (start us, length us, event | category | flops | bytes accessed | tf_op | source)
XLA Modules:
  0.0 468.6 jit_solution(7522102101981526100)
XLA Ops:
  6.5 1.4 slice.48
  7.9 1.2 slice.49
  9.1 2.0 pad_maximum_fusion.1
  11.1 1.1 copy.103
  12.3 0.5 convert_reduce_fusion
  12.8 1.0 fusion.4
  13.7 150.0 %all-gather.2.cloned.1.call-done = bf16[2048,3072]{0,1:T(8,128)(2,1)} async-done(((bf16[2048,192]{0,1:T(8,128)(2,1)}), bf16[2048,3072]{0,1:T(8,128)(2,1)}) %all-gather.2.cloned.1.call-update) | async-done | bytes 12582928 | tf_op jit(solution)/shard_map/all_gather | solution.py:51
  163.8 7.7 %fusion.11 = bf16[512,1536]{1,0:T(8,128)(2,1)S(1)} fusion(bf16[2048,3072]{0,1:T(8,128)(2,1)} %all-gather.2.cloned.1.call-done, bf16[512,3072]{1,0:T(8,128)(2,1)S(1)} %copy-done, f32[512]{0:T(512)S(1)} %add_rsqrt_fusion, f32[512]{0:T(512)S(1)} %broadcast_multiply_fusion.4), kind=kOutput, calls=%fused_computation.18 | convolution fusion | flops 4838916096 | bytes 14159872 | tf_op jit(solution)/shard_map/dot_general | solution.py:31
  171.7 1.0 copy.55
  173.0 1.0 copy.56
  174.5 0.3 multiply_reduce_fusion.1
  174.9 1.2 fusion.73
  176.1 1.5 fusion.51
  177.6 1.3 fusion.21
  178.8 1.1 fusion.36
  180.0 1.3 fusion.74
  181.3 1.4 fusion.23
  182.6 1.8 copy.67
  184.5 1.7 copy.114
  186.2 1.8 copy.69
  188.0 1.0 copy.113
  189.0 5.5 %convolution_convert_fusion.1 = bf16[512,3072]{1,0:T(8,128)(2,1)} fusion(bf16[2048,3072]{0,1:T(8,128)(2,1)} %all-gather.2.cloned.1.call-done, bf16[512,256]{1,0:T(8,128)(2,1)S(1)} %bitcast.156, bf16[512,256]{1,0:T(8,128)(2,1)} %bitcast.155), kind=kOutput, calls=%fused_computation.11 | convolution fusion | flops 1613234176 | bytes 6815744 | tf_op jit(solution)/shard_map/dot_general | solution.py:70
  194.4 4.7 %copy.70 = bf16[512,3072]{0,1:T(8,128)(2,1)} copy(bf16[512,3072]{1,0:T(8,128)(2,1)} %convolution_convert_fusion.1) | data formatting | bytes 6291456 | tf_op jit(solution)/shard_map/convert_element_type | solution.py:79
  199.2 16.2 %all-to-all-start = ((bf16[512,16,192]{0,2,1:T(8,128)(2,1)}), bf16[512,16,192]{0,2,1:T(8,128)(2,1)}, u32[]{:S(2)}, u32[]{:S(2)}) async-start(bf16[512,16,192]{0,2,1:T(8,128)(2,1)} %bitcast.143), calls=%async_computation | async-start | bytes 6291456 | tf_op jit(solution)/shard_map/all_to_all | solution.py:78
  215.4 0.8 dynamic_slice.3
  216.1 43.1 %all-to-all-done = bf16[512,16,192]{0,2,1:T(8,128)(2,1)} async-done(((bf16[512,16,192]{0,2,1:T(8,128)(2,1)}), bf16[512,16,192]{0,2,1:T(8,128)(2,1)}, u32[]{:S(2)}, u32[]{:S(2)}) %all-to-all-start) | async-done | bytes 3145760 | tf_op jit(solution)/shard_map/all_to_all | solution.py:78
  259.2 2.4 convert_reduce_fusion.1
  261.7 2.0 broadcast_in_dim.15
  263.6 6.9 %all-to-all-start.1 = ((bf16[16,512,192]{1,2,0:T(8,128)(2,1)}), bf16[16,512,192]{1,2,0:T(8,128)(2,1)}, u32[]{:S(2)}, u32[]{:S(2)}) async-start(bf16[16,512,192]{1,2,0:T(8,128)(2,1)} %broadcast_in_dim.15), calls=%async_computation.1 | async-start | bytes 6291456 | tf_op jit(solution)/shard_map/all_to_all | solution.py:85
  270.6 2.7 slice.71
  273.2 2.6 copy.71
  275.8 38.5 %all-to-all-done.1 = bf16[16,512,192]{1,2,0:T(8,128)(2,1)} async-done(((bf16[16,512,192]{1,2,0:T(8,128)(2,1)}), bf16[16,512,192]{1,2,0:T(8,128)(2,1)}, u32[]{:S(2)}, u32[]{:S(2)}) %all-to-all-start.1) | async-done | bytes 3145760 | tf_op jit(solution)/shard_map/all_to_all | solution.py:85
  314.4 5.5 %dot_general.62 = bf16[2,256,3072]{1,0,2:T(2,128)(2,1)} reshape(bf16[512,16,192]{0,2,1:T(8,128)(2,1)} %bitcast.11) | data formatting | bytes 6291456 | tf_op jit(solution)/shard_map/dot_general | solution.py:31
  319.9 3.4 fusion.17
  323.3 1.3 fusion.22
  324.6 0.7 multiply_reduce_fusion
  325.3 4.0 fusion.6
  329.3 1.0 multiply_reduce_fusion.4
  330.3 1.5 fusion.65
  332.0 0.3 fusion.49
  332.3 1.0 pad_maximum_fusion.2
  333.3 3.3 copy.79
  336.5 3.1 convert_element_type.64
  339.7 2.3 copy.80
  342.0 4.8 %convolution_convert_fusion = bf16[3072,3,256]{2,0,1:T(8,128)(2,1)S(1)} fusion(bf16[3,256,512]{2,1,0:T(8,128)(2,1)} %bitcast.154, bf16[512,3072]{1,0:T(8,128)(2,1)S(1)} %copy-done.1, f32[512]{0:T(512)S(1)} %add_rsqrt_fusion, f32[512]{0:T(512)S(1)} %broadcast_multiply_fusion.4), kind=kOutput, calls=%fused_computation.10 | convolution fusion | flops 2424569856 | bytes 8654848 | tf_op jit(solution)/shard_map/dot_general | solution.py:37
  346.8 3.2 pad_maximum_fusion
  350.0 109.5 %reduce-scatter.2.cloned.1.call-done = bf16[192,4,256]{2,0,1:T(8,128)(2,1)} async-done(((bf16[3072,4,256]{2,0,1:T(8,128)(2,1)}), bf16[192,4,256]{2,0,1:T(8,128)(2,1)}) %reduce-scatter.2.cloned.1.call-update) | async-done | bytes 393232 | tf_op jit(solution)/shard_map/reduce_scatter | solution.py:93
  459.5 2.2 copy.82
  (36 shorter events, 1.4 us)
Async XLA Ops:
  6.5 5.7 %copy-start = (bf16[512,3072]{1,0:T(8,128)(2,1)S(1)}, bf16[512,3072]{1,0:T(8,128)(2,1)}, u32[]{:S(2)}) copy-start(bf16[512,3072]{1,0:T(8,128)(2,1)} %param.4) | copy-start | bytes 9437188
  6.5 157.2 %all-gather.2.cloned.1.call-start = ((), (), s32[]{:S(2)}) async-start(), calls=%async_computation.3 | async-start | bytes 13369344 | tf_op jit(solution)/shard_map/all_gather | solution.py:51
  172.8 1.5 copy-start.2
  199.2 60.0 %all-to-all-start = ((bf16[512,16,192]{0,2,1:T(8,128)(2,1)}), bf16[512,16,192]{0,2,1:T(8,128)(2,1)}, u32[]{:S(2)}, u32[]{:S(2)}) async-start(bf16[512,16,192]{0,2,1:T(8,128)(2,1)} %bitcast.143), calls=%async_computation | async-start | bytes 6291456 | tf_op jit(solution)/shard_map/all_to_all | solution.py:78
  263.6 50.7 %all-to-all-start.1 = ((bf16[16,512,192]{1,2,0:T(8,128)(2,1)}), bf16[16,512,192]{1,2,0:T(8,128)(2,1)}, u32[]{:S(2)}, u32[]{:S(2)}) async-start(bf16[16,512,192]{1,2,0:T(8,128)(2,1)} %broadcast_in_dim.15), calls=%async_computation.1 | async-start | bytes 6291456 | tf_op jit(solution)/shard_map/all_to_all | solution.py:85
  270.5 189.0 %reduce-scatter.2.cloned.1.call-start = ((), (), s32[]{:S(2)}) async-start(), calls=%async_computation.4 | async-start | bytes 6684672 | tf_op jit(solution)/shard_map/reduce_scatter | solution.py:93
  323.3 2.0 copy-start.4
  332.3 9.7 %copy-start.1 = (bf16[512,3072]{1,0:T(8,128)(2,1)S(1)}, bf16[512,3072]{1,0:T(8,128)(2,1)}, u32[]{:S(2)}) copy-start(bf16[512,3072]{1,0:T(8,128)(2,1)} %param.4) | copy-start | bytes 9437188
  342.0 4.8 %copy-start.3 = (bf16[3072,1,256]{2,0,1:T(8,128)(2,1)S(1)}, bf16[3072,1,256]{2,0,1:T(8,128)(2,1)}, u32[]{:S(2)}) copy-start(bf16[3072,1,256]{2,0,1:T(8,128)(2,1)} %fusion.6) | copy-start | bytes 4718596
Sparse Core Ops, SparseCore 0:
  12.4 151.3 all-gather.1
  350.1 109.3 reduce-scatter.1

commit v3 on v2

--- a/solution.py
+++ b/solution.py
@@ -1,7 +1,10 @@
 import jax
 import jax.numpy as jnp
 from jax import lax
-from jax.sharding import PartitionSpec as P
+from jax.sharding import Mesh, PartitionSpec as P
+
+FSDP = ("z_hi", "x")
+TENSOR = ("z_lo", "y", "core")
 
 HEAD = 128
 PATCHES = 256
@@ -48,7 +51,7 @@
     local = jnp.concatenate(
         [weights[:, 0:3], direction[:, 0:3], weights[:, 3:4], direction[:, 3:4]], 1
     ).reshape(share_rows, 8 * head_cols)
-    gathered = lax.all_gather(local.T, "fsdp", axis=1, tiled=True)
+    gathered = lax.all_gather(local.T, FSDP, axis=1, tiled=True)
     in_both = gathered[: 6 * head_cols]
     out_both = gathered[6 * head_cols :]
     both_in = cross_rows(normed, in_both).astype(jnp.bfloat16)
@@ -73,16 +76,16 @@
         (((1,), (0,)), ((), ())),
         preferred_element_type=jnp.float32,
     )
-    n_tensor = lax.axis_size("tensor")
+    n_tensor = lax.axis_size(TENSOR)
     chunk = model_width // n_tensor
     arrived = lax.all_to_all(
-        partial_sum.astype(jnp.bfloat16).reshape(local_rows, n_tensor, chunk), "tensor", 1, 1
+        partial_sum.astype(jnp.bfloat16).reshape(local_rows, n_tensor, chunk), TENSOR, 1, 1
     )
     output_dot = jnp.sum(arrived.astype(jnp.float32), 1)
-    own_precision = lax.dynamic_slice_in_dim(precision, lax.axis_index("tensor") * chunk, chunk)
+    own_precision = lax.dynamic_slice_in_dim(precision, lax.axis_index(TENSOR) * chunk, chunk)
     cotangent_part = (own_precision * output_dot).astype(jnp.bfloat16)
     spread = jnp.broadcast_to(cotangent_part[None], (n_tensor, local_rows, chunk))
-    cotangent = jnp.moveaxis(lax.all_to_all(spread, "tensor", 0, 0), 0, 1).reshape(
+    cotangent = jnp.moveaxis(lax.all_to_all(spread, TENSOR, 0, 0), 0, 1).reshape(
         local_rows, model_width
     )
     back_rows = cross_rows(cotangent, out_both[:head_cols])
@@ -90,25 +93,30 @@
     primal_out, pullback = jax.vjp(attend, *primal_args)
     gradients = pullback(back_rows)
     stacked = jnp.stack(gradients, axis=2).reshape(local_rows, 3 * head_cols).astype(jnp.bfloat16)
-    return lax.psum_scatter(
-        jnp.concatenate(
-            [
-                over_tokens(normed, stacked).reshape(model_width, 3, head_cols),
-                over_tokens(cotangent, mixed_rows)[:, None, :],
-            ],
-            axis=1,
-        ).astype(jnp.bfloat16),
-        "fsdp",
-        scatter_dimension=0,
-        tiled=True,
-    ).astype(jnp.float32)
+    summed = jnp.concatenate(
+        [
+            over_tokens(normed, stacked).reshape(model_width, 3, head_cols),
+            over_tokens(cotangent, mixed_rows)[:, None, :],
+        ],
+        axis=1,
+    ).astype(jnp.bfloat16)
+    n_hi = lax.axis_size("z_hi")
+    n_x = lax.axis_size("x")
+    summed = summed.reshape(n_hi, n_x, share_rows, 4, head_cols).swapaxes(0, 1)
+    summed = summed.reshape(model_width, 4, head_cols)
+    summed = lax.psum_scatter(summed, "x", scatter_dimension=0, tiled=True)
+    return lax.psum_scatter(summed, "z_hi", scatter_dimension=0, tiled=True).astype(jnp.float32)
 
 
 def solution(mesh):
+    n_fsdp, n_tensor = mesh.devices.shape
+    n_x = 4 if n_fsdp % 4 == 0 else n_fsdp
+    parts = mesh.devices.reshape(n_fsdp // n_x, n_x, 2, n_tensor // 4, 2)
+    fine = Mesh(parts, ("z_hi", "x", "z_lo", "y", "core"))
     return jax.shard_map(
         body,
-        mesh=mesh,
-        in_specs=(P("fsdp", None), P("fsdp", None, "tensor"), P("fsdp", None, "tensor"), P()),
-        out_specs=P("fsdp", None, "tensor"),
+        mesh=fine,
+        in_specs=(P(FSDP, None), P(FSDP, None, TENSOR), P(FSDP, None, TENSOR), P()),
+        out_specs=P(FSDP, None, TENSOR),
         check_vma=False,
     )

time: 470 us -> 462 us (0.983)
  waiting for transfers between devices: 341 us -> 335 us
    all_gather x1, waiting for transfers between devices: 150 us -> 144 us  [body(): gathered = lax.all_gather(local.T, FSDP, axis=1, tiled=True)]
    reduce_scatter x1 -> x2, waiting for transfers between devices: 110 us -> 110 us  [the longest x1 66 us: body(): summed = lax.psum_scatter(summed, 'x', scatter_dimension=0, tiled=True)]
  transfers between devices with their start and end apart: 4 -> 5, of which waited for: 4 -> 5; matrix products, arithmetic and copies ran while one was open for 2% -> 3% of each run, Pallas kernels for 0% -> 0%
where the time goes in v3:
time: 462 us; the launch traced here: 461 us
  waiting for transfers between devices  335 us (73%)
  local copies, waits for them, and re-layouts  42.8 us (9%)
  matrix products  36.4 us (8%)
  starting transfers between devices  23.2 us (5%)
  between operations  13.4 us (3%)
  other arithmetic  10.2 us (2%)
    all_gather x1, waiting for transfers between devices, body(): gathered = lax.all_gather(local.T, FSDP, axis=1, tiled=True)  144 us
    reduce_scatter x1, waiting for transfers between devices, body(): summed = lax.psum_scatter(summed, 'x', scatter_dimension=0, tiled=True)  66 us
    reduce_scatter x1, waiting for transfers between devices, body(): lax.psum_scatter(summed, 'z_hi', scatter_dimension=0, tiled=True)  44.4 us
    all_to_all x1, waiting for transfers between devices, body(): lax.all_to_all(partial_sum.astype(jnp.bfloat16).reshape(local_rows, n_ten...  43.1 us
    all_to_all x1, waiting for transfers between devices, body(): lax.all_to_all(spread, TENSOR, 0, 0)  36.7 us
    all_to_all x1, starting transfers between devices, body(): lax.all_to_all(partial_sum.astype(jnp.bfloat16).reshape(local_rows, n_ten...  16.2 us
    dot_general x2, matrix products, cross_rows(): lax.dot_general(left, right, (((1,), (1,)), ((), ())), preferred_element_...  12.8 us
  transfers between devices with their start and end apart: 5, of which 5 were waited for; matrix products, arithmetic and copies ran while one was open for 3% of the time, Pallas kernels for 0%

profile of v3, /device:TPU:8, one launch (start us, length us, event | category | flops | bytes accessed | tf_op | source)
XLA Modules:
  0.0 460.7 jit_solution(3880986391664952742)
XLA Ops:
  6.5 1.2 slice.48
  7.8 1.2 slice.49
  9.0 2.0 pad_maximum_fusion
  11.0 1.1 copy.106
  12.1 3.2 copy.56
  15.3 0.5 convert_reduce_fusion
  15.8 0.9 fusion.4
  16.7 2.5 fusion.5
  19.1 144.5 %all-gather.2.cloned.1.call-done = bf16[2048,3072]{0,1:T(8,128)(2,1)} async-done(((bf16[2048,192]{0,1:T(8,128)(2,1)}), bf16[2048,3072]{0,1:T(8,128)(2,1)}) %all-gather.2.cloned.1.call-update) | async-done | bytes 12582928 | tf_op jit(solution)/shard_map/all_gather | solution.py:54
  163.6 9.4 %fusion.9 = bf16[512,1536]{1,0:T(8,128)(2,1)S(1)} fusion(bf16[512,3072]{0,1:T(8,128)(2,1)} %fusion.5, bf16[2048,3072]{0,1:T(8,128)(2,1)} %all-gather.2.cloned.1.call-done), kind=kOutput, calls=%fused_computation.14 | convolution fusion | flops 4832624640 | bytes 14155776 | tf_op jit(solution)/shard_map/dot_general | solution.py:34
  173.3 1.0 copy.57
  174.6 1.2 copy.58
  176.6 1.2 fusion.71
  177.8 1.5 fusion.50
  179.3 1.3 fusion.20
  180.6 1.1 fusion.35
  181.7 1.3 fusion.72
  183.0 1.4 fusion.22
  184.4 1.8 copy.69
  186.2 1.7 copy.116
  187.9 1.8 copy.71
  189.8 1.0 copy.115
  190.7 5.5 %convolution_convert_fusion = bf16[512,3072]{1,0:T(8,128)(2,1)} fusion(bf16[2048,3072]{0,1:T(8,128)(2,1)} %all-gather.2.cloned.1.call-done, bf16[512,256]{1,0:T(8,128)(2,1)S(1)} %bitcast.176, bf16[512,256]{1,0:T(8,128)(2,1)} %bitcast.175), kind=kOutput, calls=%fused_computation.10 | convolution fusion | flops 1613234176 | bytes 6815744 | tf_op jit(solution)/shard_map/dot_general | solution.py:73
  196.2 4.7 %copy.72 = bf16[512,3072]{0,1:T(8,128)(2,1)} copy(bf16[512,3072]{1,0:T(8,128)(2,1)} %convolution_convert_fusion) | data formatting | bytes 6291456 | tf_op jit(solution)/shard_map/convert_element_type | solution.py:82
  200.9 16.2 %all-to-all-start = ((bf16[512,16,192]{0,2,1:T(8,128)(2,1)}), bf16[512,16,192]{0,2,1:T(8,128)(2,1)}, u32[]{:S(2)}, u32[]{:S(2)}) async-start(bf16[512,16,192]{0,2,1:T(8,128)(2,1)} %bitcast.163), calls=%async_computation | async-start | bytes 6291456 | tf_op jit(solution)/shard_map/all_to_all | solution.py:81
  217.1 0.8 dynamic_slice.3
  217.9 43.1 %all-to-all-done = bf16[512,16,192]{0,2,1:T(8,128)(2,1)} async-done(((bf16[512,16,192]{0,2,1:T(8,128)(2,1)}), bf16[512,16,192]{0,2,1:T(8,128)(2,1)}, u32[]{:S(2)}, u32[]{:S(2)}) %all-to-all-start) | async-done | bytes 3145760 | tf_op jit(solution)/shard_map/all_to_all | solution.py:81
  261.0 2.4 convert_reduce_fusion.1
  263.4 2.0 broadcast_in_dim.12
  265.4 6.9 %all-to-all-start.1 = ((bf16[16,512,192]{1,2,0:T(8,128)(2,1)}), bf16[16,512,192]{1,2,0:T(8,128)(2,1)}, u32[]{:S(2)}, u32[]{:S(2)}) async-start(bf16[16,512,192]{1,2,0:T(8,128)(2,1)} %broadcast_in_dim.12), calls=%async_computation.1 | async-start | bytes 6291456 | tf_op jit(solution)/shard_map/all_to_all | solution.py:88
  272.3 1.8 reshape.182
  274.2 2.7 slice.71
  276.9 2.6 copy.73
  279.5 36.7 %all-to-all-done.1 = bf16[16,512,192]{1,2,0:T(8,128)(2,1)} async-done(((bf16[16,512,192]{1,2,0:T(8,128)(2,1)}), bf16[16,512,192]{1,2,0:T(8,128)(2,1)}, u32[]{:S(2)}, u32[]{:S(2)}) %all-to-all-start.1) | async-done | bytes 3145760 | tf_op jit(solution)/shard_map/all_to_all | solution.py:88
  316.1 5.5 %dot_general.74 = bf16[2,256,3072]{1,0,2:T(2,128)(2,1)} reshape(bf16[512,16,192]{0,2,1:T(8,128)(2,1)} %bitcast.14) | data formatting | bytes 6291456 | tf_op jit(solution)/shard_map/dot_general | solution.py:34
  321.7 3.4 fusion.16
  325.1 1.3 fusion.21
  326.4 0.7 multiply_reduce_fusion
  327.1 1.0 multiply_reduce_fusion.4
  328.1 1.5 fusion.65
  330.1 1.1 copy.81
  331.9 3.0 fusion.12
  334.9 2.9 convolution_convert_fusion.1
  337.8 0.5 maximum_bitcast_fusion
  338.4 3.1 copy.83
  341.5 66.0 %reduce-scatter.3.cloned.1.call-done = bf16[768,4,256]{2,0,1:T(8,128)(2,1)} async-done(((bf16[3072,4,256]{2,0,1:T(8,128)(2,1)}), bf16[768,4,256]{2,0,1:T(8,128)(2,1)}) %reduce-scatter.3.cloned.1.call-update) | async-done | bytes 1572880 | tf_op jit(solution)/shard_map/reduce_scatter | solution.py:107
  407.6 44.4 %reduce-scatter.5.cloned.1.call-done = bf16[192,4,256]{2,0,1:T(8,128)(2,1)} async-done(((bf16[768,4,256]{2,0,1:T(8,128)(2,1)}), bf16[192,4,256]{2,0,1:T(8,128)(2,1)}) %reduce-scatter.5.cloned.1.call-update) | async-done | bytes 393232 | tf_op jit(solution)/shard_map/reduce_scatter | solution.py:108
  451.9 2.2 copy.84
  (39 shorter events, 2.7 us)
Async XLA Ops:
  6.5 157.1 %all-gather.2.cloned.1.call-start = ((), (), s32[]{:S(2)}) async-start(), calls=%async_computation.4 | async-start | bytes 13369344 | tf_op jit(solution)/shard_map/all_gather | solution.py:54
  174.4 1.7 copy-start
  200.9 60.0 %all-to-all-start = ((bf16[512,16,192]{0,2,1:T(8,128)(2,1)}), bf16[512,16,192]{0,2,1:T(8,128)(2,1)}, u32[]{:S(2)}, u32[]{:S(2)}) async-start(bf16[512,16,192]{0,2,1:T(8,128)(2,1)} %bitcast.163), calls=%async_computation | async-start | bytes 6291456 | tf_op jit(solution)/shard_map/all_to_all | solution.py:81
  265.4 50.7 %all-to-all-start.1 = ((bf16[16,512,192]{1,2,0:T(8,128)(2,1)}), bf16[16,512,192]{1,2,0:T(8,128)(2,1)}, u32[]{:S(2)}, u32[]{:S(2)}) async-start(bf16[16,512,192]{1,2,0:T(8,128)(2,1)} %broadcast_in_dim.12), calls=%async_computation.1 | async-start | bytes 6291456 | tf_op jit(solution)/shard_map/all_to_all | solution.py:88
  272.3 135.3 %reduce-scatter.3.cloned.1.call-start = ((), (), s32[]{:S(2)}) async-start(), calls=%async_computation.5 | async-start | bytes 7864320 | tf_op jit(solution)/shard_map/reduce_scatter | solution.py:107
  330.0 1.9 copy-start.2
  331.9 3.0 copy-start.1
  341.5 110.5 %reduce-scatter.5.cloned.1.call-start = ((), (), s32[]{:S(2)}) async-start(), calls=%async_computation.6 | async-start | bytes 1966080 | tf_op jit(solution)/shard_map/reduce_scatter | solution.py:108
Sparse Core Ops, SparseCore 0:
  12.2 151.3 all-gather.1
  341.6 65.9 reduce-scatter.2
  410.1 41.7 reduce-scatter.4

commit v4 on v3

--- a/solution.py
+++ b/solution.py
@@ -105,7 +105,10 @@
     summed = summed.reshape(n_hi, n_x, share_rows, 4, head_cols).swapaxes(0, 1)
     summed = summed.reshape(model_width, 4, head_cols)
     summed = lax.psum_scatter(summed, "x", scatter_dimension=0, tiled=True)
-    return lax.psum_scatter(summed, "z_hi", scatter_dimension=0, tiled=True).astype(jnp.float32)
+    arrived_rows = lax.all_to_all(
+        summed.reshape(n_hi, share_rows, 4, head_cols), "z_hi", 0, 0
+    )
+    return jnp.sum(arrived_rows.astype(jnp.float32), 0)
 
 
 def solution(mesh):

time: 462 us -> 464 us (level)
  blocking collectives: 0 us -> 45.9 us
  waiting for transfers between devices: 335 us -> 290 us
    all_to_all x0 -> x1, blocking collectives: none -> 45.9 us  [body(): lax.all_to_all(summed.reshape(n_hi, share_rows, 4, head_cols), 'z_hi', 0, 0)]
    reduce_scatter x1 -> x0, waiting for transfers between devices: 44.4 us -> none  [body(): lax.psum_scatter(summed, 'z_hi', scatter_dimension=0, tiled=True)]
  transfers between devices with their start and end apart: 5 -> 4, of which waited for: 5 -> 4; matrix products, arithmetic and copies ran while one was open for 3% -> 3% of each run, Pallas kernels for 0% -> 0%
where the time goes in v4:
time: 464 us; the launch traced here: 463 us
  waiting for transfers between devices  290 us (62%)
  blocking collectives  45.9 us (10%)
  local copies, waits for them, and re-layouts  43.5 us (9%)
  matrix products  36.4 us (8%)
  starting transfers between devices  23.1 us (5%)
  between operations  13.7 us (3%)
  other arithmetic  10.4 us (2%)
    all_gather x1, waiting for transfers between devices, body(): gathered = lax.all_gather(local.T, FSDP, axis=1, tiled=True)  144 us
    reduce_scatter x1, waiting for transfers between devices, body(): summed = lax.psum_scatter(summed, 'x', scatter_dimension=0, tiled=True)  66.1 us
    all_to_all x1, blocking collectives, body(): lax.all_to_all(summed.reshape(n_hi, share_rows, 4, head_cols), 'z_hi', 0, 0)  45.9 us
    all_to_all x1, waiting for transfers between devices, body(): lax.all_to_all(partial_sum.astype(jnp.bfloat16).reshape(local_rows, n_ten...  43.1 us
    all_to_all x1, waiting for transfers between devices, body(): lax.all_to_all(spread, TENSOR, 0, 0)  36.7 us
    all_to_all x1, starting transfers between devices, body(): lax.all_to_all(partial_sum.astype(jnp.bfloat16).reshape(local_rows, n_ten...  16.2 us
    dot_general x2, matrix products, cross_rows(): lax.dot_general(left, right, (((1,), (1,)), ((), ())), preferred_element_...  12.8 us
  transfers between devices with their start and end apart: 4, of which 4 were waited for; matrix products, arithmetic and copies ran while one was open for 3% of the time, Pallas kernels for 0%

profile of v4, /device:TPU:8, one launch (start us, length us, event | category | flops | bytes accessed | tf_op | source)
XLA Modules:
  0.0 463.5 jit_solution(789463137165313387)
XLA Ops:
  6.5 1.2 slice.48
  7.8 1.2 slice.49
  9.0 2.0 pad_maximum_fusion
  11.0 1.1 copy.108
  12.1 3.2 copy.55
  15.8 0.9 fusion.4
  16.7 2.5 fusion.5
  19.1 144.5 %all-gather.2.cloned.1.call-done = bf16[2048,3072]{0,1:T(8,128)(2,1)} async-done(((bf16[2048,192]{0,1:T(8,128)(2,1)}), bf16[2048,3072]{0,1:T(8,128)(2,1)}) %all-gather.2.cloned.1.call-update) | async-done | bytes 12582928 | tf_op jit(solution)/shard_map/all_gather | solution.py:54
  163.6 9.4 %fusion.9 = bf16[512,1536]{1,0:T(8,128)(2,1)S(1)} fusion(bf16[512,3072]{0,1:T(8,128)(2,1)} %fusion.5, bf16[2048,3072]{0,1:T(8,128)(2,1)} %all-gather.2.cloned.1.call-done), kind=kOutput, calls=%fused_computation.15 | convolution fusion | flops 4832624640 | bytes 14155776 | tf_op jit(solution)/shard_map/dot_general | solution.py:34
  173.3 1.0 copy.56
  174.6 1.2 copy.57
  176.6 1.2 fusion.71
  177.8 1.5 fusion.50
  179.3 1.3 fusion.20
  180.6 1.1 fusion.35
  181.7 1.3 fusion.72
  183.0 1.4 fusion.22
  184.4 1.8 copy.68
  186.2 1.7 copy.118
  187.9 1.8 copy.70
  189.8 1.0 copy.117
  190.7 5.5 %convolution_convert_fusion = bf16[512,3072]{1,0:T(8,128)(2,1)} fusion(bf16[2048,3072]{0,1:T(8,128)(2,1)} %all-gather.2.cloned.1.call-done, bf16[512,256]{1,0:T(8,128)(2,1)S(1)} %bitcast.178, bf16[512,256]{1,0:T(8,128)(2,1)} %bitcast.177), kind=kOutput, calls=%fused_computation.10 | convolution fusion | flops 1613234176 | bytes 6815744 | tf_op jit(solution)/shard_map/dot_general | solution.py:73
  196.2 4.7 %copy.71 = bf16[512,3072]{0,1:T(8,128)(2,1)} copy(bf16[512,3072]{1,0:T(8,128)(2,1)} %convolution_convert_fusion) | data formatting | bytes 6291456 | tf_op jit(solution)/shard_map/convert_element_type | solution.py:82
  200.9 16.2 %all-to-all-start = ((bf16[512,16,192]{0,2,1:T(8,128)(2,1)}), bf16[512,16,192]{0,2,1:T(8,128)(2,1)}, u32[]{:S(2)}, u32[]{:S(2)}) async-start(bf16[512,16,192]{0,2,1:T(8,128)(2,1)} %bitcast.164), calls=%async_computation | async-start | bytes 6291456 | tf_op jit(solution)/shard_map/all_to_all | solution.py:81
  217.1 0.8 dynamic_slice.3
  217.9 43.1 %all-to-all-done = bf16[512,16,192]{0,2,1:T(8,128)(2,1)} async-done(((bf16[512,16,192]{0,2,1:T(8,128)(2,1)}), bf16[512,16,192]{0,2,1:T(8,128)(2,1)}, u32[]{:S(2)}, u32[]{:S(2)}) %all-to-all-start) | async-done | bytes 3145760 | tf_op jit(solution)/shard_map/all_to_all | solution.py:81
  261.0 2.4 convert_reduce_fusion.1
  263.4 2.0 broadcast_in_dim.12
  265.4 6.9 %all-to-all-start.1 = ((bf16[16,512,192]{1,2,0:T(8,128)(2,1)}), bf16[16,512,192]{1,2,0:T(8,128)(2,1)}, u32[]{:S(2)}, u32[]{:S(2)}) async-start(bf16[16,512,192]{1,2,0:T(8,128)(2,1)} %broadcast_in_dim.12), calls=%async_computation.1 | async-start | bytes 6291456 | tf_op jit(solution)/shard_map/all_to_all | solution.py:88
  272.3 1.8 reshape.186
  274.2 2.7 slice.71
  276.9 2.6 copy.72
  279.5 36.7 %all-to-all-done.1 = bf16[16,512,192]{1,2,0:T(8,128)(2,1)} async-done(((bf16[16,512,192]{1,2,0:T(8,128)(2,1)}), bf16[16,512,192]{1,2,0:T(8,128)(2,1)}, u32[]{:S(2)}, u32[]{:S(2)}) %all-to-all-start.1) | async-done | bytes 3145760 | tf_op jit(solution)/shard_map/all_to_all | solution.py:88
  316.1 5.5 %dot_general.74 = bf16[2,256,3072]{1,0,2:T(2,128)(2,1)} reshape(bf16[512,16,192]{0,2,1:T(8,128)(2,1)} %bitcast.14) | data formatting | bytes 6291456 | tf_op jit(solution)/shard_map/dot_general | solution.py:34
  321.7 3.4 fusion.16
  325.1 1.3 fusion.21
  326.4 0.7 multiply_reduce_fusion
  327.1 1.0 multiply_reduce_fusion.4
  328.1 1.5 fusion.65
  330.1 1.1 copy.80
  331.9 3.0 fusion.12
  334.9 2.9 convolution_convert_fusion.1
  337.8 0.5 maximum_bitcast_fusion
  338.4 3.1 copy.82
  341.5 66.1 %reduce-scatter.2.cloned.1.call-done = bf16[768,4,256]{2,0,1:T(8,128)(2,1)} async-done(((bf16[3072,4,256]{2,0,1:T(8,128)(2,1)}), bf16[768,4,256]{2,0,1:T(8,128)(2,1)}) %reduce-scatter.2.cloned.1.call-update) | async-done | bytes 1572880 | tf_op jit(solution)/shard_map/reduce_scatter | solution.py:107
  407.6 1.5 copy.83
  409.1 45.9 %all_to_all.15 = bf16[4,192,4,256]{3,1,2,0:T(8,128)(2,1)S(1)} all-to-all(bf16[4,192,4,256]{3,1,2,0:T(8,128)(2,1)S(1)} %copy.83), channel_id=1, replica_groups=mesh['z_hi'=4,'x'=4,'z_lo'=2,'y'=4,'core'=2] {'z_hi'}, dimensions={0} | all-to-all | bytes 3145728 | tf_op jit(solution)/shard_map/all_to_all | solution.py:108
  455.3 1.4 copy.85
  (39 shorter events, 3.4 us)
Async XLA Ops:
  6.5 157.1 %all-gather.2.cloned.1.call-start = ((), (), s32[]{:S(2)}) async-start(), calls=%async_computation.4 | async-start | bytes 13369344 | tf_op jit(solution)/shard_map/all_gather | solution.py:54
  174.4 1.7 copy-start
  200.9 60.0 %all-to-all-start = ((bf16[512,16,192]{0,2,1:T(8,128)(2,1)}), bf16[512,16,192]{0,2,1:T(8,128)(2,1)}, u32[]{:S(2)}, u32[]{:S(2)}) async-start(bf16[512,16,192]{0,2,1:T(8,128)(2,1)} %bitcast.164), calls=%async_computation | async-start | bytes 6291456 | tf_op jit(solution)/shard_map/all_to_all | solution.py:81
  265.4 50.7 %all-to-all-start.1 = ((bf16[16,512,192]{1,2,0:T(8,128)(2,1)}), bf16[16,512,192]{1,2,0:T(8,128)(2,1)}, u32[]{:S(2)}, u32[]{:S(2)}) async-start(bf16[16,512,192]{1,2,0:T(8,128)(2,1)} %broadcast_in_dim.12), calls=%async_computation.1 | async-start | bytes 6291456 | tf_op jit(solution)/shard_map/all_to_all | solution.py:88
  272.3 135.3 %reduce-scatter.2.cloned.1.call-start = ((), (), s32[]{:S(2)}) async-start(), calls=%async_computation.5 | async-start | bytes 7864320 | tf_op jit(solution)/shard_map/reduce_scatter | solution.py:107
  330.0 1.9 copy-start.2
  331.9 3.0 copy-start.1
Sparse Core Ops, SparseCore 0:
  12.2 151.3 all-gather.1
  341.6 65.9 reduce-scatter.1

commit v5 on v3

--- a/solution.py
+++ b/solution.py
@@ -70,25 +70,26 @@
     mixed, mixed_dot = jax.jvp(attend, primal_args, tangent_args)
     mixed_rows = mixed.reshape(local_rows, head_cols).astype(jnp.bfloat16)
     tangent_out = mixed_dot.reshape(local_rows, head_cols).astype(jnp.bfloat16)
-    partial_sum = lax.dot_general(
+    partial_cols = lax.dot_general(
+        out_both,
         jnp.concatenate([tangent_out, mixed_rows], 1),
-        out_both,
-        (((1,), (0,)), ((), ())),
+        (((0,), (1,)), ((), ())),
         preferred_element_type=jnp.float32,
     )
     n_tensor = lax.axis_size(TENSOR)
     chunk = model_width // n_tensor
     arrived = lax.all_to_all(
-        partial_sum.astype(jnp.bfloat16).reshape(local_rows, n_tensor, chunk), TENSOR, 1, 1
+        partial_cols.astype(jnp.bfloat16).reshape(n_tensor, chunk, local_rows), TENSOR, 0, 0
     )
-    output_dot = jnp.sum(arrived.astype(jnp.float32), 1)
+    output_dot = jnp.sum(arrived.astype(jnp.float32), 0)
     own_precision = lax.dynamic_slice_in_dim(precision, lax.axis_index(TENSOR) * chunk, chunk)
-    cotangent_part = (own_precision * output_dot).astype(jnp.bfloat16)
-    spread = jnp.broadcast_to(cotangent_part[None], (n_tensor, local_rows, chunk))
-    cotangent = jnp.moveaxis(lax.all_to_all(spread, TENSOR, 0, 0), 0, 1).reshape(
-        local_rows, model_width
+    cotangent_part = (own_precision[:, None] * output_dot).astype(jnp.bfloat16)
+    spread = jnp.broadcast_to(cotangent_part[None], (n_tensor, chunk, local_rows))
+    cotangent_cols = lax.all_to_all(spread, TENSOR, 0, 0).reshape(model_width, local_rows)
+    back_rows = lax.dot_general(
+        cotangent_cols, out_both[:head_cols], (((0,), (1,)), ((), ())),
+        preferred_element_type=jnp.float32,
     )
-    back_rows = cross_rows(cotangent, out_both[:head_cols])
     back_rows = back_rows.reshape(local_rows // PATCHES, PATCHES, head_cols // HEAD, HEAD)
     primal_out, pullback = jax.vjp(attend, *primal_args)
     gradients = pullback(back_rows)
@@ -96,7 +97,7 @@
     summed = jnp.concatenate(
         [
             over_tokens(normed, stacked).reshape(model_width, 3, head_cols),
-            over_tokens(cotangent, mixed_rows)[:, None, :],
+            jnp.dot(cotangent_cols, mixed_rows, preferred_element_type=jnp.float32)[:, None, :],
         ],
         axis=1,
     ).astype(jnp.bfloat16)

time: 462 us -> 456 us (0.987)
  local copies, waits for them, and re-layouts: 42.8 us -> 37.3 us
    dot_general x1 -> x3, matrix products: 5.48 us -> 11.8 us  [the longest x1 5.41 us: body(): lax.dot_general(out_both, jnp.concatenate([tangent_out, mixed_rows], 1),...]
    convert_element_type x1 -> x0, local copies, waits for them, and re-layouts: 4.69 us -> none  [body(): partial_sum.astype(jnp.bfloat16).reshape(local_rows, n_tensor, chunk)]
    dot_general x2 -> x1, matrix products: 12.8 us -> 9.42 us  [cross_rows(): lax.dot_general(left, right, (((1,), (1,)), ((), ())), preferred_element_...]
where the time goes in v5:
time: 456 us; the launch traced here: 455 us
  waiting for transfers between devices  335 us (73%)
  local copies, waits for them, and re-layouts  37.3 us (8%)
  matrix products  36.3 us (8%)
  starting transfers between devices  23.2 us (5%)
  between operations  13.4 us (3%)
  other arithmetic  10.2 us (2%)
    all_gather x1, waiting for transfers between devices, body(): gathered = lax.all_gather(local.T, FSDP, axis=1, tiled=True)  144 us
    reduce_scatter x1, waiting for transfers between devices, body(): summed = lax.psum_scatter(summed, 'x', scatter_dimension=0, tiled=True)  66 us
    reduce_scatter x1, waiting for transfers between devices, body(): lax.psum_scatter(summed, 'z_hi', scatter_dimension=0, tiled=True)  44.4 us
    all_to_all x1, waiting for transfers between devices, body(): lax.all_to_all(partial_cols.astype(jnp.bfloat16).reshape(n_tensor, chunk,...  43.1 us
    all_to_all x1, waiting for transfers between devices, body(): lax.all_to_all(spread, TENSOR, 0, 0).reshape(model_width, local_rows)  36.7 us
    all_to_all x1, starting transfers between devices, body(): lax.all_to_all(partial_cols.astype(jnp.bfloat16).reshape(n_tensor, chunk,...  16.2 us
    dot_general x1, matrix products, cross_rows(): lax.dot_general(left, right, (((1,), (1,)), ((), ())), preferred_element_...  9.42 us
  transfers between devices with their start and end apart: 5, of which 5 were waited for; matrix products, arithmetic and copies ran while one was open for 3% of the time, Pallas kernels for 0%

profile of v5, /device:TPU:8, one launch (start us, length us, event | category | flops | bytes accessed | tf_op | source)
XLA Modules:
  0.0 455.0 jit_solution(4592516743113283007)
XLA Ops:
  6.5 1.2 slice.48
  7.8 1.2 slice.49
  9.0 2.0 pad_maximum_fusion
  11.0 1.1 copy.102
  12.1 3.2 copy.55
  15.3 0.5 convert_reduce_fusion
  15.8 0.9 fusion.4
  16.7 2.5 fusion.5
  19.1 144.5 %all-gather.2.cloned.1.call-done = bf16[2048,3072]{0,1:T(8,128)(2,1)} async-done(((bf16[2048,192]{0,1:T(8,128)(2,1)}), bf16[2048,3072]{0,1:T(8,128)(2,1)}) %all-gather.2.cloned.1.call-update) | async-done | bytes 12582928 | tf_op jit(solution)/shard_map/all_gather | solution.py:54
  163.6 9.4 %fusion.7 = bf16[512,1536]{1,0:T(8,128)(2,1)S(1)} fusion(bf16[512,3072]{0,1:T(8,128)(2,1)} %fusion.5, bf16[2048,3072]{0,1:T(8,128)(2,1)} %all-gather.2.cloned.1.call-done), kind=kOutput, calls=%fused_computation.12 | convolution fusion | flops 4832624640 | bytes 14155776 | tf_op jit(solution)/shard_map/dot_general | solution.py:34
  173.3 1.0 copy.56
  174.6 1.2 copy.57
  176.6 1.2 fusion.66
  177.8 1.5 fusion.45
  179.3 1.3 fusion.15
  180.6 1.1 fusion.30
  181.7 1.3 fusion.67
  183.0 1.4 fusion.17
  184.4 1.8 copy.68
  186.2 1.7 copy.108
  187.9 1.8 copy.70
  189.8 1.0 copy.107
  190.7 5.4 %convolution_convert_fusion = bf16[3072,512]{1,0:T(8,128)(2,1)} fusion(bf16[2048,3072]{0,1:T(8,128)(2,1)} %all-gather.2.cloned.1.call-done, bf16[512,256]{1,0:T(8,128)(2,1)S(1)} %bitcast.176, bf16[512,256]{1,0:T(8,128)(2,1)} %bitcast.175), kind=kOutput, calls=%fused_computation.10 | convolution fusion | flops 1613234176 | bytes 6815744 | tf_op jit(solution)/shard_map/dot_general | solution.py:73
  196.2 16.2 %all-to-all-start = ((bf16[16,192,512]{2,1,0:T(8,128)(2,1)}), bf16[16,192,512]{2,1,0:T(8,128)(2,1)}, u32[]{:S(2)}, u32[]{:S(2)}) async-start(bf16[16,192,512]{2,1,0:T(8,128)(2,1)} %bitcast.163), calls=%async_computation | async-start | bytes 6291456 | tf_op jit(solution)/shard_map/all_to_all | solution.py:81
  212.4 0.8 dynamic_slice.3
  213.1 43.1 %all-to-all-done = bf16[16,192,512]{2,1,0:T(8,128)(2,1)} async-done(((bf16[16,192,512]{2,1,0:T(8,128)(2,1)}), bf16[16,192,512]{2,1,0:T(8,128)(2,1)}, u32[]{:S(2)}, u32[]{:S(2)}) %all-to-all-start) | async-done | bytes 3145760 | tf_op jit(solution)/shard_map/all_to_all | solution.py:81
  256.2 2.4 convert_reduce_fusion.1
  258.7 2.0 broadcast_in_dim.12
  260.7 6.9 %all-to-all-start.1 = ((bf16[16,192,512]{2,1,0:T(8,128)(2,1)}), bf16[16,192,512]{2,1,0:T(8,128)(2,1)}, u32[]{:S(2)}, u32[]{:S(2)}) async-start(bf16[16,192,512]{2,1,0:T(8,128)(2,1)} %broadcast_in_dim.12), calls=%async_computation.1 | async-start | bytes 6291456 | tf_op jit(solution)/shard_map/all_to_all | solution.py:88
  267.6 1.8 reshape.178
  269.4 2.7 slice.71
  272.1 2.6 copy.72
  274.7 36.7 %all-to-all-done.1 = bf16[16,192,512]{2,1,0:T(8,128)(2,1)} async-done(((bf16[16,192,512]{2,1,0:T(8,128)(2,1)}), bf16[16,192,512]{2,1,0:T(8,128)(2,1)}, u32[]{:S(2)}, u32[]{:S(2)}) %all-to-all-start.1) | async-done | bytes 3145760 | tf_op jit(solution)/shard_map/all_to_all | solution.py:88
  311.4 4.6 %copy.71 = bf16[512,3072]{1,0:T(8,128)(2,1)} copy(bf16[512,3072]{0,1:T(8,128)(2,1)} %bitcast.15) | data formatting | bytes 6291456 | tf_op jit(solution)/shard_map/dot_general | solution.py:89
  316.0 3.4 convolution_bitcast_fusion.2
  319.4 1.3 fusion.16
  320.7 0.7 multiply_reduce_fusion
  321.4 1.0 multiply_reduce_fusion.4
  322.4 1.5 fusion.60
  324.5 1.1 copy.79
  325.6 0.4 convert_element_type.65
  326.2 3.0 fusion.10
  329.3 2.9 convolution_convert_fusion.1
  332.2 0.5 maximum_bitcast_fusion
  332.7 3.1 copy.81
  335.9 66.0 %reduce-scatter.3.cloned.1.call-done = bf16[768,4,256]{2,0,1:T(8,128)(2,1)} async-done(((bf16[3072,4,256]{2,0,1:T(8,128)(2,1)}), bf16[768,4,256]{2,0,1:T(8,128)(2,1)}) %reduce-scatter.3.cloned.1.call-update) | async-done | bytes 1572880 | tf_op jit(solution)/shard_map/reduce_scatter | solution.py:108
  401.9 44.4 %reduce-scatter.5.cloned.1.call-done = bf16[192,4,256]{2,0,1:T(8,128)(2,1)} async-done(((bf16[768,4,256]{2,0,1:T(8,128)(2,1)}), bf16[192,4,256]{2,0,1:T(8,128)(2,1)}) %reduce-scatter.5.cloned.1.call-update) | async-done | bytes 393232 | tf_op jit(solution)/shard_map/reduce_scatter | solution.py:109
  446.3 2.2 copy.82
  (38 shorter events, 2.3 us)
Async XLA Ops:
  6.5 157.1 %all-gather.2.cloned.1.call-start = ((), (), s32[]{:S(2)}) async-start(), calls=%async_computation.4 | async-start | bytes 13369344 | tf_op jit(solution)/shard_map/all_gather | solution.py:54
  174.4 1.7 copy-start
  196.2 60.0 %all-to-all-start = ((bf16[16,192,512]{2,1,0:T(8,128)(2,1)}), bf16[16,192,512]{2,1,0:T(8,128)(2,1)}, u32[]{:S(2)}, u32[]{:S(2)}) async-start(bf16[16,192,512]{2,1,0:T(8,128)(2,1)} %bitcast.163), calls=%async_computation | async-start | bytes 6291456 | tf_op jit(solution)/shard_map/all_to_all | solution.py:81
  260.7 50.7 %all-to-all-start.1 = ((bf16[16,192,512]{2,1,0:T(8,128)(2,1)}), bf16[16,192,512]{2,1,0:T(8,128)(2,1)}, u32[]{:S(2)}, u32[]{:S(2)}) async-start(bf16[16,192,512]{2,1,0:T(8,128)(2,1)} %broadcast_in_dim.12), calls=%async_computation.1 | async-start | bytes 6291456 | tf_op jit(solution)/shard_map/all_to_all | solution.py:88
  267.5 134.4 %reduce-scatter.3.cloned.1.call-start = ((), (), s32[]{:S(2)}) async-start(), calls=%async_computation.5 | async-start | bytes 7864320 | tf_op jit(solution)/shard_map/reduce_scatter | solution.py:108
  324.4 1.9 copy-start.2
  326.2 3.0 copy-start.1
  335.8 110.5 %reduce-scatter.5.cloned.1.call-start = ((), (), s32[]{:S(2)}) async-start(), calls=%async_computation.6 | async-start | bytes 1966080 | tf_op jit(solution)/shard_map/reduce_scatter | solution.py:109
Sparse Core Ops, SparseCore 0:
  12.2 151.3 all-gather.1
  335.9 65.9 reduce-scatter.2
  404.5 41.7 reduce-scatter.4

commit v6 on v5

--- a/solution.py
+++ b/solution.py
@@ -78,14 +78,24 @@
     )
     n_tensor = lax.axis_size(TENSOR)
     chunk = model_width // n_tensor
-    arrived = lax.all_to_all(
-        partial_cols.astype(jnp.bfloat16).reshape(n_tensor, chunk, local_rows), TENSOR, 0, 0
+    n_core = lax.axis_size("core")
+    n_chip = n_tensor // n_core
+    by_core = (
+        partial_cols.astype(jnp.bfloat16)
+        .reshape(n_chip, n_core, chunk, local_rows)
+        .swapaxes(0, 1)
     )
+    pair_sum = jnp.sum(lax.all_to_all(by_core, "core", 0, 0).astype(jnp.float32), 0)
+    arrived = lax.all_to_all(pair_sum.astype(jnp.bfloat16), ("z_lo", "y"), 0, 0)
     output_dot = jnp.sum(arrived.astype(jnp.float32), 0)
     own_precision = lax.dynamic_slice_in_dim(precision, lax.axis_index(TENSOR) * chunk, chunk)
     cotangent_part = (own_precision[:, None] * output_dot).astype(jnp.bfloat16)
-    spread = jnp.broadcast_to(cotangent_part[None], (n_tensor, chunk, local_rows))
-    cotangent_cols = lax.all_to_all(spread, TENSOR, 0, 0).reshape(model_width, local_rows)
+    spread = jnp.broadcast_to(cotangent_part[None], (n_chip, chunk, local_rows))
+    on_chip = lax.all_to_all(spread, ("z_lo", "y"), 0, 0)
+    spread = jnp.broadcast_to(on_chip[None], (n_core, n_chip, chunk, local_rows))
+    cotangent_cols = (
+        lax.all_to_all(spread, "core", 0, 0).swapaxes(0, 1).reshape(model_width, local_rows)
+    )
     back_rows = lax.dot_general(
         cotangent_cols, out_both[:head_cols], (((0,), (1,)), ((), ())),
         preferred_element_type=jnp.float32,

time: 456 us -> 430 us (0.943)
  waiting for transfers between devices: 335 us -> 284 us
  blocking collectives: 0 us -> 13.5 us
  local copies, waits for them, and re-layouts: 37.3 us -> 48.7 us
    all_to_all x2, waiting for transfers between devices: 79.7 us -> 31.4 us  [the longest x1 18.9 us: body(): arrived = lax.all_to_all(pair_sum.astype(jnp.bfloat16), ('z_lo', 'y'), 0, 0)]
    all_to_all x0 -> x2, blocking collectives: none -> 13.5 us  [the longest x1 7.22 us: body(): lax.all_to_all(by_core, 'core', 0, 0).astype(jnp.float32)]
where the time goes in v6:
time: 430 us; the launch traced here: 428 us
  waiting for transfers between devices  284 us (66%)
  local copies, waits for them, and re-layouts  48.7 us (11%)
  matrix products  32.6 us (8%)
  starting transfers between devices  21.6 us (5%)
  other arithmetic  14.5 us (3%)
  blocking collectives  13.5 us (3%)
  between operations  13.4 us (3%)
    all_gather x1, waiting for transfers between devices, body(): gathered = lax.all_gather(local.T, FSDP, axis=1, tiled=True)  144 us
    reduce_scatter x1, waiting for transfers between devices, body(): summed = lax.psum_scatter(summed, 'x', scatter_dimension=0, tiled=True)  63.9 us
    reduce_scatter x1, waiting for transfers between devices, body(): lax.psum_scatter(summed, 'z_hi', scatter_dimension=0, tiled=True)  44.4 us
    all_to_all x1, waiting for transfers between devices, body(): arrived = lax.all_to_all(pair_sum.astype(jnp.bfloat16), ('z_lo', 'y'), 0, 0)  18.9 us
    all_to_all x1, starting transfers between devices, body(): arrived = lax.all_to_all(pair_sum.astype(jnp.bfloat16), ('z_lo', 'y'), 0, 0)  16.2 us
    all_to_all x1, waiting for transfers between devices, body(): on_chip = lax.all_to_all(spread, ('z_lo', 'y'), 0, 0)  12.5 us
    dot_general x1, matrix products, cross_rows(): lax.dot_general(left, right, (((1,), (1,)), ((), ())), preferred_element_...  9.42 us
  transfers between devices with their start and end apart: 5, of which 5 were waited for; matrix products, arithmetic and copies ran while one was open for 3% of the time, Pallas kernels for 0%

profile of v6, /device:TPU:8, one launch (start us, length us, event | category | flops | bytes accessed | tf_op | source)
XLA Modules:
  0.0 428.4 jit_solution(11656200164103643073)
XLA Ops:
  6.5 1.2 slice.48
  7.8 1.2 slice.49
  9.0 2.0 pad_maximum_fusion
  11.0 1.1 copy.134
  12.1 3.2 copy.85
  16.7 2.5 fusion.5
  19.1 144.5 %all-gather.2.cloned.1.call-done = bf16[2048,3072]{0,1:T(8,128)(2,1)} async-done(((bf16[2048,192]{0,1:T(8,128)(2,1)}), bf16[2048,3072]{0,1:T(8,128)(2,1)}) %all-gather.2.cloned.1.call-update) | async-done | bytes 12582928 | tf_op jit(solution)/shard_map/all_gather | solution.py:54
  163.6 9.4 %fusion.7 = bf16[512,1536]{1,0:T(8,128)(2,1)S(1)} fusion(bf16[512,3072]{0,1:T(8,128)(2,1)} %fusion.5, bf16[2048,3072]{0,1:T(8,128)(2,1)} %all-gather.2.cloned.1.call-done), kind=kOutput, calls=%fused_computation.13 | convolution fusion | flops 4832624640 | bytes 14155776 | tf_op jit(solution)/shard_map/dot_general | solution.py:34
  173.3 1.0 copy.86
  174.6 1.2 copy.87
  176.6 1.2 fusion.66
  177.8 1.5 fusion.45
  179.3 1.3 fusion.15
  180.6 1.1 fusion.30
  181.7 1.3 fusion.67
  183.0 1.4 fusion.17
  184.4 1.8 copy.98
  186.2 1.7 copy.142
  187.9 1.8 copy.100
  189.8 1.0 copy.141
  190.7 3.7 convolution_convert_fusion
  194.8 7.2 %all_to_all.20 = bf16[2,8,192,512]{3,2,1,0:T(8,128)(2,1)} all-to-all(bf16[2,8,192,512]{3,2,1,0:T(8,128)(2,1)S(1)} %bitcast.171), channel_id=1, replica_groups=mesh['z_hi'=4,'x'=4,'z_lo'=2,'y'=4,'core'=2] {'core'}, dimensions={0} | all-to-all | bytes 6291456 | tf_op jit(solution)/shard_map/all_to_all | solution.py:88
  202.0 4.1 reduce_sum.191
  206.1 16.2 %all-to-all-start.1 = ((bf16[8,192,512]{2,1,0:T(8,128)(2,1)}), bf16[8,192,512]{2,1,0:T(8,128)(2,1)}, u32[]{:S(2)}, u32[]{:S(2)}) async-start(bf16[8,192,512]{2,1,0:T(8,128)(2,1)} %reduce_sum.191), calls=%async_computation.1 | async-start | bytes 3145728 | tf_op jit(solution)/shard_map/all_to_all | solution.py:89
  223.1 18.9 %all-to-all-done.1 = bf16[8,192,512]{2,1,0:T(8,128)(2,1)} async-done(((bf16[8,192,512]{2,1,0:T(8,128)(2,1)}), bf16[8,192,512]{2,1,0:T(8,128)(2,1)}, u32[]{:S(2)}, u32[]{:S(2)}) %all-to-all-start.1) | async-done | bytes 1572896 | tf_op jit(solution)/shard_map/all_to_all | solution.py:89
  242.0 1.7 convert_reduce_fusion.1
  243.7 1.3 broadcast_in_dim.14
  245.1 5.3 %all-to-all-start.2 = ((bf16[8,192,512]{2,1,0:T(8,128)(2,1)}), bf16[8,192,512]{2,1,0:T(8,128)(2,1)}, u32[]{:S(2)}, u32[]{:S(2)}) async-start(bf16[8,192,512]{2,1,0:T(8,128)(2,1)} %broadcast_in_dim.14), calls=%async_computation.2 | async-start | bytes 3145728 | tf_op jit(solution)/shard_map/all_to_all | solution.py:94
  250.4 1.8 reshape.179
  252.2 2.7 slice.71
  254.9 2.6 copy.104
  257.5 12.5 %all-to-all-done.2 = bf16[8,192,512]{2,1,0:T(8,128)(2,1)} async-done(((bf16[8,192,512]{2,1,0:T(8,128)(2,1)}), bf16[8,192,512]{2,1,0:T(8,128)(2,1)}, u32[]{:S(2)}, u32[]{:S(2)}) %all-to-all-start.2) | async-done | bytes 1572896 | tf_op jit(solution)/shard_map/all_to_all | solution.py:94
  269.9 1.8 broadcast_in_dim.15
  271.7 6.3 %all_to_all.21 = bf16[2,8,192,512]{3,2,1,0:T(8,128)(2,1)S(1)} all-to-all(bf16[2,8,192,512]{3,2,1,0:T(8,128)(2,1)S(1)} %broadcast_in_dim.15), channel_id=1, replica_groups=mesh['z_hi'=4,'x'=4,'z_lo'=2,'y'=4,'core'=2] {'core'}, dimensions={0} | all-to-all | bytes 6291456 | tf_op jit(solution)/shard_map/all_to_all | solution.py:97
  278.0 1.9 copy.102
  279.9 4.7 %copy.103 = bf16[512,3072]{1,0:T(8,128)(2,1)} copy(bf16[512,3072]{0,1:T(8,128)(2,1)} %bitcast.168) | data formatting | bytes 6291456 | tf_op jit(solution)/shard_map/dot_general | solution.py:99
  284.6 3.4 convolution_bitcast_fusion.2
  288.0 1.3 fusion.16
  290.0 1.0 multiply_reduce_fusion.4
  291.0 1.5 fusion.60
  293.9 3.4 copy.111
  297.3 3.1 convert_element_type.67
  300.5 2.3 copy.112
  304.8 2.9 convolution_convert_fusion.1
  308.3 3.1 copy.113
  311.4 63.9 %reduce-scatter.3.cloned.1.call-done = bf16[768,4,256]{2,0,1:T(8,128)(2,1)} async-done(((bf16[3072,4,256]{2,0,1:T(8,128)(2,1)}), bf16[768,4,256]{2,0,1:T(8,128)(2,1)}) %reduce-scatter.3.cloned.1.call-update) | async-done | bytes 1572880 | tf_op jit(solution)/shard_map/reduce_scatter | solution.py:118
  375.4 44.4 %reduce-scatter.5.cloned.1.call-done = bf16[192,4,256]{2,0,1:T(8,128)(2,1)} async-done(((bf16[768,4,256]{2,0,1:T(8,128)(2,1)}), bf16[192,4,256]{2,0,1:T(8,128)(2,1)}) %reduce-scatter.5.cloned.1.call-update) | async-done | bytes 393232 | tf_op jit(solution)/shard_map/reduce_scatter | solution.py:119
  419.7 2.2 copy.114
  (48 shorter events, 8.6 us)
Async XLA Ops:
  6.5 157.1 %all-gather.2.cloned.1.call-start = ((), (), s32[]{:S(2)}) async-start(), calls=%async_computation.6 | async-start | bytes 13369344 | tf_op jit(solution)/shard_map/all_gather | solution.py:54
  174.4 1.7 copy-start.1
  206.1 35.8 %all-to-all-start.1 = ((bf16[8,192,512]{2,1,0:T(8,128)(2,1)}), bf16[8,192,512]{2,1,0:T(8,128)(2,1)}, u32[]{:S(2)}, u32[]{:S(2)}) async-start(bf16[8,192,512]{2,1,0:T(8,128)(2,1)} %reduce_sum.191), calls=%async_computation.1 | async-start | bytes 3145728 | tf_op jit(solution)/shard_map/all_to_all | solution.py:89
  245.1 24.9 %all-to-all-start.2 = ((bf16[8,192,512]{2,1,0:T(8,128)(2,1)}), bf16[8,192,512]{2,1,0:T(8,128)(2,1)}, u32[]{:S(2)}, u32[]{:S(2)}) async-start(bf16[8,192,512]{2,1,0:T(8,128)(2,1)} %broadcast_in_dim.14), calls=%async_computation.2 | async-start | bytes 3145728 | tf_op jit(solution)/shard_map/all_to_all | solution.py:94
  250.4 124.9 %reduce-scatter.3.cloned.1.call-start = ((), (), s32[]{:S(2)}) async-start(), calls=%async_computation.7 | async-start | bytes 7864320 | tf_op jit(solution)/shard_map/reduce_scatter | solution.py:118
  292.9 9.8 %copy-start = (bf16[2,8,192,512]{3,2,0,1:T(8,128)(2,1)S(1)}, bf16[2,8,192,512]{3,2,0,1:T(8,128)(2,1)}, u32[]{:S(2)}) copy-start(bf16[2,8,192,512]{3,2,0,1:T(8,128)(2,1)} %copy.102) | copy-start | bytes 9437188
  292.9 9.8 %copy-start.3 = (bf16[512,256,1,1]{1,0,2,3:T(8,128)(2,1)S(1)}, bf16[512,256,1,1]{1,0,2,3:T(8,128)(2,1)}, u32[]{:S(2)}) copy-start(bf16[512,256,1,1]{1,0,2,3:T(8,128)(2,1)} %reshape.179) | copy-start | bytes 786436
  302.7 1.9 copy-start.2
  302.7 2.1 copy-start.4
  311.4 108.4 %reduce-scatter.5.cloned.1.call-start = ((), (), s32[]{:S(2)}) async-start(), calls=%async_computation.8 | async-start | bytes 1966080 | tf_op jit(solution)/shard_map/reduce_scatter | solution.py:119
Sparse Core Ops, SparseCore 0:
  12.2 151.3 all-gather.1
  311.5 63.8 reduce-scatter.2
  377.9 41.7 reduce-scatter.4

commit v7 on v6

--- a/solution.py
+++ b/solution.py
@@ -115,8 +115,10 @@
     n_x = lax.axis_size("x")
     summed = summed.reshape(n_hi, n_x, share_rows, 4, head_cols).swapaxes(0, 1)
     summed = summed.reshape(model_width, 4, head_cols)
-    summed = lax.psum_scatter(summed, "x", scatter_dimension=0, tiled=True)
-    return lax.psum_scatter(summed, "z_hi", scatter_dimension=0, tiled=True).astype(jnp.float32)
+    arrived_x = lax.all_to_all(summed.reshape(n_x, n_hi * share_rows, 4, head_cols), "x", 0, 0)
+    summed = jnp.sum(arrived_x.astype(jnp.float32), 0).astype(jnp.bfloat16)
+    arrived_rows = lax.all_to_all(summed.reshape(n_hi, share_rows, 4, head_cols), "z_hi", 0, 0)
+    return jnp.sum(arrived_rows.astype(jnp.float32), 0)
 
 
 def solution(mesh):

time: 430 us -> 440 us (1.023)
  blocking collectives: 13.5 us -> 126 us
  waiting for transfers between devices: 284 us -> 176 us
    all_to_all x0 -> x2, blocking collectives: none -> 113 us  [the longest x1 75.8 us: body(): lax.all_to_all(summed.reshape(n_x, n_hi * share_rows, 4, head_cols), 'x',...]
    reduce_scatter x2 -> x0, waiting for transfers between devices: 108 us -> none  [the longest x1 63.9 us: body(): summed = lax.psum_scatter(summed, 'x', scatter_dimension=0, tiled=True)]
  transfers between devices with their start and end apart: 5 -> 3, of which waited for: 5 -> 3; matrix products, arithmetic and copies ran while one was open for 3% -> 3% of each run, Pallas kernels for 0% -> 0%
where the time goes in v7:
time: 440 us; the launch traced here: 434 us
  waiting for transfers between devices  176 us (40%)
  blocking collectives  126 us (29%)
  local copies, waits for them, and re-layouts  45.7 us (10%)
  matrix products  32.6 us (7%)
  starting transfers between devices  21.5 us (5%)
  other arithmetic  18.7 us (4%)
  between operations  13.7 us (3%)
    all_gather x1, waiting for transfers between devices, body(): gathered = lax.all_gather(local.T, FSDP, axis=1, tiled=True)  144 us
    all_to_all x1, blocking collectives, body(): lax.all_to_all(summed.reshape(n_x, n_hi * share_rows, 4, head_cols), 'x',...  75.8 us
    all_to_all x1, blocking collectives, body(): lax.all_to_all(summed.reshape(n_hi, share_rows, 4, head_cols), 'z_hi', 0, 0)  36.9 us
    all_to_all x1, waiting for transfers between devices, body(): arrived = lax.all_to_all(pair_sum.astype(jnp.bfloat16), ('z_lo', 'y'), 0, 0)  18.9 us
    all_to_all x1, starting transfers between devices, body(): arrived = lax.all_to_all(pair_sum.astype(jnp.bfloat16), ('z_lo', 'y'), 0, 0)  16.2 us
    all_to_all x1, waiting for transfers between devices, body(): on_chip = lax.all_to_all(spread, ('z_lo', 'y'), 0, 0)  12.5 us
    dot_general x1, matrix products, cross_rows(): lax.dot_general(left, right, (((1,), (1,)), ((), ())), preferred_element_...  9.42 us
  transfers between devices with their start and end apart: 3, of which 3 were waited for; matrix products, arithmetic and copies ran while one was open for 3% of the time, Pallas kernels for 0%

profile of v7, /device:TPU:8, one launch (start us, length us, event | category | flops | bytes accessed | tf_op | source)
XLA Modules:
  0.0 434.2 jit_solution(17572755689462693308)
XLA Ops:
  6.5 1.2 slice.48
  7.8 1.2 slice.49
  9.0 2.0 pad_maximum_fusion
  11.0 1.1 copy.167
  12.1 3.2 copy.115
  16.7 2.5 fusion.5
  19.1 144.5 %all-gather.2.cloned.1.call-done = bf16[2048,3072]{0,1:T(8,128)(2,1)} async-done(((bf16[2048,192]{0,1:T(8,128)(2,1)}), bf16[2048,3072]{0,1:T(8,128)(2,1)}) %all-gather.2.cloned.1.call-update) | async-done | bytes 12582928 | tf_op jit(solution)/shard_map/all_gather | solution.py:54
  163.6 9.4 %fusion.7 = bf16[512,1536]{1,0:T(8,128)(2,1)S(1)} fusion(bf16[512,3072]{0,1:T(8,128)(2,1)} %fusion.5, bf16[2048,3072]{0,1:T(8,128)(2,1)} %all-gather.2.cloned.1.call-done), kind=kOutput, calls=%fused_computation.14 | convolution fusion | flops 4832624640 | bytes 14155776 | tf_op jit(solution)/shard_map/dot_general | solution.py:34
  173.3 1.0 copy.116
  174.6 1.2 copy.117
  176.6 1.2 fusion.66
  177.8 1.5 fusion.45
  179.3 1.3 fusion.15
  180.6 1.1 fusion.30
  181.7 1.3 fusion.67
  183.0 1.4 fusion.17
  184.4 1.8 copy.128
  186.2 1.7 copy.175
  187.9 1.8 copy.130
  189.8 1.0 copy.174
  190.7 3.7 convolution_convert_fusion
  194.8 7.2 %all_to_all.30 = bf16[2,8,192,512]{3,2,1,0:T(8,128)(2,1)} all-to-all(bf16[2,8,192,512]{3,2,1,0:T(8,128)(2,1)S(1)} %bitcast.172), channel_id=1, replica_groups=mesh['z_hi'=4,'x'=4,'z_lo'=2,'y'=4,'core'=2] {'core'}, dimensions={0} | all-to-all | bytes 6291456 | tf_op jit(solution)/shard_map/all_to_all | solution.py:88
  202.0 4.1 reduce_sum.216
  206.1 16.2 %all-to-all-start.1 = ((bf16[8,192,512]{2,1,0:T(8,128)(2,1)}), bf16[8,192,512]{2,1,0:T(8,128)(2,1)}, u32[]{:S(2)}, u32[]{:S(2)}) async-start(bf16[8,192,512]{2,1,0:T(8,128)(2,1)} %reduce_sum.216), calls=%async_computation.1 | async-start | bytes 3145728 | tf_op jit(solution)/shard_map/all_to_all | solution.py:89
  223.1 18.9 %all-to-all-done.1 = bf16[8,192,512]{2,1,0:T(8,128)(2,1)} async-done(((bf16[8,192,512]{2,1,0:T(8,128)(2,1)}), bf16[8,192,512]{2,1,0:T(8,128)(2,1)}, u32[]{:S(2)}, u32[]{:S(2)}) %all-to-all-start.1) | async-done | bytes 1572896 | tf_op jit(solution)/shard_map/all_to_all | solution.py:89
  242.0 1.7 convert_reduce_fusion.2
  243.7 1.3 broadcast_in_dim.14
  245.1 5.3 %all-to-all-start.2 = ((bf16[8,192,512]{2,1,0:T(8,128)(2,1)}), bf16[8,192,512]{2,1,0:T(8,128)(2,1)}, u32[]{:S(2)}, u32[]{:S(2)}) async-start(bf16[8,192,512]{2,1,0:T(8,128)(2,1)} %broadcast_in_dim.14), calls=%async_computation.2 | async-start | bytes 3145728 | tf_op jit(solution)/shard_map/all_to_all | solution.py:94
  250.4 1.8 reshape.179
  252.2 2.7 slice.71
  254.9 2.6 copy.134
  257.5 12.5 %all-to-all-done.2 = bf16[8,192,512]{2,1,0:T(8,128)(2,1)} async-done(((bf16[8,192,512]{2,1,0:T(8,128)(2,1)}), bf16[8,192,512]{2,1,0:T(8,128)(2,1)}, u32[]{:S(2)}, u32[]{:S(2)}) %all-to-all-start.2) | async-done | bytes 1572896 | tf_op jit(solution)/shard_map/all_to_all | solution.py:94
  269.9 1.8 broadcast_in_dim.15
  271.7 6.3 %all_to_all.31 = bf16[2,8,192,512]{3,2,1,0:T(8,128)(2,1)S(1)} all-to-all(bf16[2,8,192,512]{3,2,1,0:T(8,128)(2,1)S(1)} %broadcast_in_dim.15), channel_id=1, replica_groups=mesh['z_hi'=4,'x'=4,'z_lo'=2,'y'=4,'core'=2] {'core'}, dimensions={0} | all-to-all | bytes 6291456 | tf_op jit(solution)/shard_map/all_to_all | solution.py:97
  278.0 1.9 copy.132
  279.9 4.7 %copy.133 = bf16[512,3072]{1,0:T(8,128)(2,1)} copy(bf16[512,3072]{0,1:T(8,128)(2,1)} %bitcast.169) | data formatting | bytes 6291456 | tf_op jit(solution)/shard_map/dot_general | solution.py:99
  284.6 3.4 convolution_bitcast_fusion.2
  288.0 1.3 fusion.16
  290.0 1.0 multiply_reduce_fusion.4
  291.0 1.5 fusion.60
  293.9 3.4 copy.141
  297.3 3.1 convert_element_type.69
  300.5 2.3 copy.142
  304.8 2.9 convolution_convert_fusion.1
  309.0 75.8 %all_to_all.32 = bf16[4,768,4,256]{3,1,2,0:T(8,128)(2,1)} all-to-all(bf16[4,768,4,256]{3,1,2,0:T(8,128)(2,1)S(1)} %bitcast.171), channel_id=1, replica_groups=mesh['z_hi'=4,'x'=4,'z_lo'=2,'y'=4,'core'=2] {'x'}, dimensions={0} | all-to-all | bytes 12582912 | tf_op jit(solution)/shard_map/all_to_all | solution.py:118
  384.7 4.0 reduce_sum.254
  388.8 36.9 %all_to_all.33 = bf16[4,192,4,256]{3,1,2,0:T(8,128)(2,1)S(1)} all-to-all(bf16[4,192,4,256]{3,1,2,0:T(8,128)(2,1)S(1)} %copy.144), channel_id=1, replica_groups=mesh['z_hi'=4,'x'=4,'z_lo'=2,'y'=4,'core'=2] {'z_hi'}, dimensions={0} | all-to-all | bytes 3145728 | tf_op jit(solution)/shard_map/all_to_all | solution.py:120
  425.9 1.4 copy.146
  (47 shorter events, 9.6 us)
Async XLA Ops:
  6.5 157.1 %all-gather.2.cloned.1.call-start = ((), (), s32[]{:S(2)}) async-start(), calls=%async_computation.6 | async-start | bytes 13369344 | tf_op jit(solution)/shard_map/all_gather | solution.py:54
  174.4 1.7 copy-start.1
  206.1 35.8 %all-to-all-start.1 = ((bf16[8,192,512]{2,1,0:T(8,128)(2,1)}), bf16[8,192,512]{2,1,0:T(8,128)(2,1)}, u32[]{:S(2)}, u32[]{:S(2)}) async-start(bf16[8,192,512]{2,1,0:T(8,128)(2,1)} %reduce_sum.216), calls=%async_computation.1 | async-start | bytes 3145728 | tf_op jit(solution)/shard_map/all_to_all | solution.py:89
  245.1 24.9 %all-to-all-start.2 = ((bf16[8,192,512]{2,1,0:T(8,128)(2,1)}), bf16[8,192,512]{2,1,0:T(8,128)(2,1)}, u32[]{:S(2)}, u32[]{:S(2)}) async-start(bf16[8,192,512]{2,1,0:T(8,128)(2,1)} %broadcast_in_dim.14), calls=%async_computation.2 | async-start | bytes 3145728 | tf_op jit(solution)/shard_map/all_to_all | solution.py:94
  292.9 9.8 %copy-start = (bf16[2,8,192,512]{3,2,0,1:T(8,128)(2,1)S(1)}, bf16[2,8,192,512]{3,2,0,1:T(8,128)(2,1)}, u32[]{:S(2)}) copy-start(bf16[2,8,192,512]{3,2,0,1:T(8,128)(2,1)} %copy.132) | copy-start | bytes 9437188
  292.9 9.8 %copy-start.3 = (bf16[512,256,1,1]{1,0,2,3:T(8,128)(2,1)S(1)}, bf16[512,256,1,1]{1,0,2,3:T(8,128)(2,1)}, u32[]{:S(2)}) copy-start(bf16[512,256,1,1]{1,0,2,3:T(8,128)(2,1)} %reshape.179) | copy-start | bytes 786436
  302.7 1.9 copy-start.2
  302.7 2.1 copy-start.4
Sparse Core Ops, SparseCore 0:
  12.2 151.3 all-gather.1

commit v8 on v6

--- a/solution.py
+++ b/solution.py
@@ -80,22 +80,24 @@
     chunk = model_width // n_tensor
     n_core = lax.axis_size("core")
     n_chip = n_tensor // n_core
-    by_core = (
-        partial_cols.astype(jnp.bfloat16)
-        .reshape(n_chip, n_core, chunk, local_rows)
-        .swapaxes(0, 1)
-    )
-    pair_sum = jnp.sum(lax.all_to_all(by_core, "core", 0, 0).astype(jnp.float32), 0)
+    swap = [(0, 1), (1, 0)]
+    core_index = lax.axis_index("core")
+    by_core = partial_cols.astype(jnp.bfloat16).reshape(n_chip, n_core, chunk, local_rows)
+    kept = lax.dynamic_index_in_dim(by_core, core_index, 1, keepdims=False)
+    given = lax.dynamic_index_in_dim(by_core, 1 - core_index, 1, keepdims=False)
+    received = lax.ppermute(given, "core", swap)
+    pair_sum = kept.astype(jnp.float32) + received.astype(jnp.float32)
     arrived = lax.all_to_all(pair_sum.astype(jnp.bfloat16), ("z_lo", "y"), 0, 0)
     output_dot = jnp.sum(arrived.astype(jnp.float32), 0)
     own_precision = lax.dynamic_slice_in_dim(precision, lax.axis_index(TENSOR) * chunk, chunk)
     cotangent_part = (own_precision[:, None] * output_dot).astype(jnp.bfloat16)
     spread = jnp.broadcast_to(cotangent_part[None], (n_chip, chunk, local_rows))
     on_chip = lax.all_to_all(spread, ("z_lo", "y"), 0, 0)
-    spread = jnp.broadcast_to(on_chip[None], (n_core, n_chip, chunk, local_rows))
-    cotangent_cols = (
-        lax.all_to_all(spread, "core", 0, 0).swapaxes(0, 1).reshape(model_width, local_rows)
-    )
+    partner = lax.ppermute(on_chip, "core", swap)
+    first = core_index == 0
+    cotangent_cols = jnp.stack(
+        [jnp.where(first, on_chip, partner), jnp.where(first, partner, on_chip)], 1
+    ).reshape(model_width, local_rows)
     back_rows = lax.dot_general(
         cotangent_cols, out_both[:head_cols], (((0,), (1,)), ((), ())),
         preferred_element_type=jnp.float32,

time: 430 us -> 425 us (0.988)
  blocking collectives: 13.5 us -> 24.5 us
  waiting for transfers between devices: 284 us -> 275 us
  starting transfers between devices: 21.6 us -> 16.2 us
  local copies, waits for them, and re-layouts: 48.7 us -> 44.2 us
    all_to_all x1 -> x0, waiting for transfers between devices: 12.5 us -> none  [body(): on_chip = lax.all_to_all(spread, ('z_lo', 'y'), 0, 0)]
    all_to_all x2 -> x1, blocking collectives: 13.5 us -> 24.5 us  [body(): on_chip = lax.all_to_all(spread, ('z_lo', 'y'), 0, 0)]
    all_to_all x1 -> x0, starting transfers between devices: 5.33 us -> none  [body(): on_chip = lax.all_to_all(spread, ('z_lo', 'y'), 0, 0)]
    unnamed x14 -> x16, local copies, waits for them, and re-layouts: 8.04 us -> 8.76 us
  transfers between devices with their start and end apart: 5 -> 6, of which waited for: 5 -> 5; matrix products, arithmetic and copies ran while one was open for 3% -> 4% of each run, Pallas kernels for 0% -> 0%
where the time goes in v8:
time: 425 us; the launch traced here: 423 us
  waiting for transfers between devices  275 us (65%)
  local copies, waits for them, and re-layouts  44.2 us (10%)
  matrix products  32.6 us (8%)
  blocking collectives  24.5 us (6%)
  other arithmetic  17.1 us (4%)
  starting transfers between devices  16.2 us (4%)
  between operations  13.4 us (3%)
    all_gather x1, waiting for transfers between devices, body(): gathered = lax.all_gather(local.T, FSDP, axis=1, tiled=True)  144 us
    reduce_scatter x1, waiting for transfers between devices, body(): summed = lax.psum_scatter(summed, 'x', scatter_dimension=0, tiled=True)  63.8 us
    reduce_scatter x1, waiting for transfers between devices, body(): lax.psum_scatter(summed, 'z_hi', scatter_dimension=0, tiled=True)  44.4 us
    all_to_all x1, blocking collectives, body(): on_chip = lax.all_to_all(spread, ('z_lo', 'y'), 0, 0)  24.5 us
    all_to_all x1, waiting for transfers between devices, body(): arrived = lax.all_to_all(pair_sum.astype(jnp.bfloat16), ('z_lo', 'y'), 0, 0)  18.9 us
    all_to_all x1, starting transfers between devices, body(): arrived = lax.all_to_all(pair_sum.astype(jnp.bfloat16), ('z_lo', 'y'), 0, 0)  16.2 us
    dot_general x1, matrix products, cross_rows(): lax.dot_general(left, right, (((1,), (1,)), ((), ())), preferred_element_...  9.42 us
    unnamed x16, local copies, waits for them, and re-layouts  8.76 us
  transfers between devices with their start and end apart: 6, of which 5 were waited for; matrix products, arithmetic and copies ran while one was open for 4% of the time, Pallas kernels for 0%

profile of v8, /device:TPU:8, one launch (start us, length us, event | category | flops | bytes accessed | tf_op | source)
XLA Modules:
  0.0 423.4 jit_solution(13196525194503101645)
XLA Ops:
  6.5 1.2 slice.48
  7.8 1.2 slice.49
  9.0 2.0 pad_maximum_fusion.1
  11.0 1.1 copy.105
  12.1 3.2 copy.57
  16.7 2.5 fusion.5
  19.1 144.5 %all-gather.2.cloned.1.call-done = bf16[2048,3072]{0,1:T(8,128)(2,1)} async-done(((bf16[2048,192]{0,1:T(8,128)(2,1)}), bf16[2048,3072]{0,1:T(8,128)(2,1)}) %all-gather.2.cloned.1.call-update) | async-done | bytes 12582928 | tf_op jit(solution)/shard_map/all_gather | solution.py:54
  163.6 9.4 %fusion.10 = bf16[512,1536]{1,0:T(8,128)(2,1)S(1)} fusion(bf16[512,3072]{0,1:T(8,128)(2,1)} %fusion.5, bf16[2048,3072]{0,1:T(8,128)(2,1)} %all-gather.2.cloned.1.call-done), kind=kOutput, calls=%fused_computation.17 | convolution fusion | flops 4832624640 | bytes 14155776 | tf_op jit(solution)/shard_map/dot_general | solution.py:34
  173.3 1.0 copy.58
  174.6 1.2 copy.59
  176.6 1.2 fusion.74
  177.8 1.5 fusion.53
  179.3 1.3 fusion.23
  180.6 1.1 fusion.38
  181.7 1.3 fusion.75
  183.0 1.4 fusion.25
  184.4 1.8 copy.70
  186.2 1.7 copy.111
  187.9 1.8 copy.72
  189.8 1.0 copy.110
  190.7 3.7 convolution_convert_fusion
  194.5 1.4 dynamic-slice_bitcast_fusion
  196.7 3.7 collective-permute-done
  200.4 3.5 fusion.7
  203.9 16.2 %all-to-all-start = ((bf16[8,192,512]{2,1,0:T(8,128)(2,1)}), bf16[8,192,512]{2,1,0:T(8,128)(2,1)}, u32[]{:S(2)}, u32[]{:S(2)}) async-start(bf16[8,192,512]{2,1,0:T(8,128)(2,1)} %fusion.7), calls=%async_computation | async-start | bytes 3145728 | tf_op jit(solution)/shard_map/all_to_all | solution.py:90
  220.9 18.9 %all-to-all-done = bf16[8,192,512]{2,1,0:T(8,128)(2,1)} async-done(((bf16[8,192,512]{2,1,0:T(8,128)(2,1)}), bf16[8,192,512]{2,1,0:T(8,128)(2,1)}, u32[]{:S(2)}, u32[]{:S(2)}) %all-to-all-start) | async-done | bytes 1572896 | tf_op jit(solution)/shard_map/all_to_all | solution.py:90
  239.8 1.7 convert_reduce_fusion.1
  241.7 24.5 %all_to_all.10 = bf16[8,192,512]{2,1,0:T(8,128)(2,1)} all-to-all(bf16[8,192,512]{2,1,0:T(8,128)(2,1)S(1)} %broadcast_in_dim.12), channel_id=1, replica_groups=mesh['z_hi'=4,'x'=4,'z_lo'=2,'y'=4,'core'=2] {'z_lo','y'}, dimensions={0} | all-to-all | bytes 3145728 | tf_op jit(solution)/shard_map/all_to_all | solution.py:95
  266.2 1.8 reshape.181
  268.0 2.7 slice.71
  270.7 2.6 copy.75
  273.3 2.1 select_bitcast_fusion.1
  275.4 2.0 pad_maximum_fusion
  277.3 4.7 %copy.74 = bf16[512,3072]{1,0:T(8,128)(2,1)} copy(bf16[512,3072]{0,1:T(8,128)(2,1)} %bitcast.180) | data formatting | bytes 6291456 | tf_op jit(solution)/shard_map/dot_general | solution.py:101
  282.0 3.4 convolution_bitcast_fusion.2
  285.4 1.3 fusion.24
  287.4 1.0 multiply_reduce_fusion.4
  288.4 1.5 fusion.68
  290.5 1.8 copy.82
  292.3 3.3 convert_element_type.81
  295.5 2.3 copy.83
  297.8 1.0 fusion.16
  298.8 0.9 copy-done.3
  299.9 2.9 convolution_convert_fusion.1
  303.4 3.1 copy.84
  306.5 63.8 %reduce-scatter.3.cloned.1.call-done = bf16[768,4,256]{2,0,1:T(8,128)(2,1)} async-done(((bf16[3072,4,256]{2,0,1:T(8,128)(2,1)}), bf16[768,4,256]{2,0,1:T(8,128)(2,1)}) %reduce-scatter.3.cloned.1.call-update) | async-done | bytes 1572880 | tf_op jit(solution)/shard_map/reduce_scatter | solution.py:120
  370.3 44.4 %reduce-scatter.5.cloned.1.call-done = bf16[192,4,256]{2,0,1:T(8,128)(2,1)} async-done(((bf16[768,4,256]{2,0,1:T(8,128)(2,1)}), bf16[192,4,256]{2,0,1:T(8,128)(2,1)}) %reduce-scatter.5.cloned.1.call-update) | async-done | bytes 393232 | tf_op jit(solution)/shard_map/reduce_scatter | solution.py:121
  414.7 2.2 copy.85
  (51 shorter events, 6.4 us)
Async XLA Ops:
  6.5 157.1 %all-gather.2.cloned.1.call-start = ((), (), s32[]{:S(2)}) async-start(), calls=%async_computation.4 | async-start | bytes 13369344 | tf_op jit(solution)/shard_map/all_gather | solution.py:54
  174.4 1.7 copy-start.2
  194.5 2.2 copy-start.1
  196.7 3.8 collective-permute-start
  203.9 35.8 %all-to-all-start = ((bf16[8,192,512]{2,1,0:T(8,128)(2,1)}), bf16[8,192,512]{2,1,0:T(8,128)(2,1)}, u32[]{:S(2)}, u32[]{:S(2)}) async-start(bf16[8,192,512]{2,1,0:T(8,128)(2,1)} %fusion.7), calls=%async_computation | async-start | bytes 3145728 | tf_op jit(solution)/shard_map/all_to_all | solution.py:90
  220.1 150.1 %reduce-scatter.3.cloned.1.call-start = ((), (), s32[]{:S(2)}) async-start(), calls=%async_computation.5 | async-start | bytes 7864320 | tf_op jit(solution)/shard_map/reduce_scatter | solution.py:120
  266.2 7.1 %collective-permute-start.1 = (bf16[8,192,512]{2,1,0:T(8,128)(2,1)}, bf16[8,192,512]{2,1,0:T(8,128)(2,1)}, u32[]{:S(2)}, u32[]{:S(2)}) collective-permute-start(bf16[8,192,512]{2,1,0:T(8,128)(2,1)} %all_to_all.10), channel_id=1, source_target_pairs={{0,1},{1,0},{2,3},{3,2},{4,5},{5,4},{6,7},{7,6},{8,9},{9,8},{10,11... | collective-permute-start | bytes 4718600 | tf_op jit(solution)/shard_map/ppermute | solution.py:96
  290.4 7.4 %copy-start.4 = (bf16[512,256,1,1]{1,0,2,3:T(8,128)(2,1)S(1)}, bf16[512,256,1,1]{1,0,2,3:T(8,128)(2,1)}, u32[]{:S(2)}) copy-start(bf16[512,256,1,1]{1,0,2,3:T(8,128)(2,1)} %reshape.181) | copy-start | bytes 786436
  292.3 5.6 %copy-start = (bf16[8,2,192,512]{3,2,1,0:T(8,128)(2,1)S(1)}, bf16[8,2,192,512]{3,2,1,0:T(8,128)(2,1)}, u32[]{:S(2)}) copy-start(bf16[8,2,192,512]{3,2,1,0:T(8,128)(2,1)} %pad_maximum_fusion) | copy-start | bytes 9437188
  297.8 1.9 copy-start.3
  297.8 2.1 copy-start.5
  306.4 108.2 %reduce-scatter.5.cloned.1.call-start = ((), (), s32[]{:S(2)}) async-start(), calls=%async_computation.6 | async-start | bytes 1966080 | tf_op jit(solution)/shard_map/reduce_scatter | solution.py:121
Sparse Core Ops, SparseCore 0:
  12.2 151.3 all-gather.1
  306.6 63.6 reduce-scatter.2
  372.8 41.7 reduce-scatter.4

commit v9 on v8

--- a/solution.py
+++ b/solution.py
@@ -118,7 +118,14 @@
     summed = summed.reshape(n_hi, n_x, share_rows, 4, head_cols).swapaxes(0, 1)
     summed = summed.reshape(model_width, 4, head_cols)
     summed = lax.psum_scatter(summed, "x", scatter_dimension=0, tiled=True)
-    return lax.psum_scatter(summed, "z_hi", scatter_dimension=0, tiled=True).astype(jnp.float32)
+    blocks = summed.reshape(n_hi, share_rows, 4, head_cols)
+    hi_index = lax.axis_index("z_hi")
+    total = lax.dynamic_index_in_dim(blocks, hi_index, 0, keepdims=False).astype(jnp.float32)
+    for shift in range(1, n_hi):
+        outgoing = lax.dynamic_index_in_dim(blocks, (hi_index + shift) % n_hi, 0, keepdims=False)
+        pairs = [(i, (i + shift) % n_hi) for i in range(n_hi)]
+        total = total + lax.ppermute(outgoing, "z_hi", pairs).astype(jnp.float32)
+    return total
 
 
 def solution(mesh):

time: 425 us -> 424 us (level)
  waiting for transfers between devices: 275 us -> 262 us
  starting transfers between devices: 16.2 us -> 26.1 us
    reduce_scatter x1 -> x0, waiting for transfers between devices: 44.4 us -> none  [body(): lax.psum_scatter(summed, 'z_hi', scatter_dimension=0, tiled=True)]
    ppermute x0 -> x3, waiting for transfers between devices: none -> 31.4 us  [body(): total = total + lax.ppermute(outgoing, 'z_hi', pairs).astype(jnp.float32)]
    ppermute x0 -> x3, starting transfers between devices: none -> 9.93 us  [body(): total = total + lax.ppermute(outgoing, 'z_hi', pairs).astype(jnp.float32)]
  transfers between devices with their start and end apart: 6 -> 8, of which waited for: 5 -> 7; matrix products, arithmetic and copies ran while one was open for 4% -> 4% of each run, Pallas kernels for 0% -> 0%
where the time goes in v9:
time: 424 us; the launch traced here: 423 us
  waiting for transfers between devices  262 us (62%)
  local copies, waits for them, and re-layouts  44.5 us (10%)
  matrix products  32.8 us (8%)
  starting transfers between devices  26.1 us (6%)
  blocking collectives  24.5 us (6%)
  other arithmetic  18.5 us (4%)
  between operations  13.8 us (3%)
    all_gather x1, waiting for transfers between devices, body(): gathered = lax.all_gather(local.T, FSDP, axis=1, tiled=True)  144 us
    reduce_scatter x1, waiting for transfers between devices, body(): summed = lax.psum_scatter(summed, 'x', scatter_dimension=0, tiled=True)  63.8 us
    ppermute x3, waiting for transfers between devices, body(): total = total + lax.ppermute(outgoing, 'z_hi', pairs).astype(jnp.float32)  31.4 us
    all_to_all x1, blocking collectives, body(): on_chip = lax.all_to_all(spread, ('z_lo', 'y'), 0, 0)  24.5 us
    all_to_all x1, waiting for transfers between devices, body(): arrived = lax.all_to_all(pair_sum.astype(jnp.bfloat16), ('z_lo', 'y'), 0, 0)  18.9 us
    all_to_all x1, starting transfers between devices, body(): arrived = lax.all_to_all(pair_sum.astype(jnp.bfloat16), ('z_lo', 'y'), 0, 0)  16.2 us
    ppermute x3, starting transfers between devices, body(): total = total + lax.ppermute(outgoing, 'z_hi', pairs).astype(jnp.float32)  9.93 us
    dot_general x1, matrix products, cross_rows(): lax.dot_general(left, right, (((1,), (1,)), ((), ())), preferred_element_...  9.42 us
  transfers between devices with their start and end apart: 8, of which 7 were waited for; matrix products, arithmetic and copies ran while one was open for 4% of the time, Pallas kernels for 0%

profile of v9, /device:TPU:8, one launch (start us, length us, event | category | flops | bytes accessed | tf_op | source)
XLA Modules:
  0.0 422.6 jit_solution(6205364730576592801)
XLA Ops:
  6.5 1.2 slice.48
  7.8 1.2 slice.49
  9.0 2.0 pad_maximum_fusion.1
  12.1 3.2 copy.60
  16.7 2.5 fusion.5
  19.1 144.5 %all-gather.2.cloned.1.call-done = bf16[2048,3072]{0,1:T(8,128)(2,1)} async-done(((bf16[2048,192]{0,1:T(8,128)(2,1)}), bf16[2048,3072]{0,1:T(8,128)(2,1)}) %all-gather.2.cloned.1.call-update) | async-done | bytes 12582928 | tf_op jit(solution)/shard_map/all_gather | solution.py:54
  163.6 9.4 %fusion.10 = bf16[512,1536]{1,0:T(8,128)(2,1)S(1)} fusion(bf16[512,3072]{0,1:T(8,128)(2,1)} %fusion.5, bf16[2048,3072]{0,1:T(8,128)(2,1)} %all-gather.2.cloned.1.call-done), kind=kOutput, calls=%fused_computation.17 | convolution fusion | flops 4832624640 | bytes 14155776 | tf_op jit(solution)/shard_map/dot_general | solution.py:34
  174.6 1.2 copy.62
  176.6 1.2 fusion.76
  177.8 1.5 fusion.55
  179.3 1.3 fusion.23
  180.6 1.1 fusion.40
  181.7 1.3 fusion.77
  183.0 1.4 fusion.25
  184.4 1.8 copy.73
  186.2 1.7 copy.127
  187.9 1.8 copy.75
  190.7 3.7 convolution_convert_fusion
  194.5 1.4 dynamic-slice_bitcast_fusion
  196.7 3.7 collective-permute-done
  200.4 3.5 fusion.7
  203.9 16.2 %all-to-all-start = ((bf16[8,192,512]{2,1,0:T(8,128)(2,1)}), bf16[8,192,512]{2,1,0:T(8,128)(2,1)}, u32[]{:S(2)}, u32[]{:S(2)}) async-start(bf16[8,192,512]{2,1,0:T(8,128)(2,1)} %fusion.7), calls=%async_computation | async-start | bytes 3145728 | tf_op jit(solution)/shard_map/all_to_all | solution.py:90
  220.9 18.9 %all-to-all-done = bf16[8,192,512]{2,1,0:T(8,128)(2,1)} async-done(((bf16[8,192,512]{2,1,0:T(8,128)(2,1)}), bf16[8,192,512]{2,1,0:T(8,128)(2,1)}, u32[]{:S(2)}, u32[]{:S(2)}) %all-to-all-start) | async-done | bytes 1572896 | tf_op jit(solution)/shard_map/all_to_all | solution.py:90
  239.8 1.7 convert_reduce_fusion.1
  241.7 24.5 %all_to_all.10 = bf16[8,192,512]{2,1,0:T(8,128)(2,1)} all-to-all(bf16[8,192,512]{2,1,0:T(8,128)(2,1)S(1)} %broadcast_in_dim.12), channel_id=1, replica_groups=mesh['z_hi'=4,'x'=4,'z_lo'=2,'y'=4,'core'=2] {'z_lo','y'}, dimensions={0} | all-to-all | bytes 3145728 | tf_op jit(solution)/shard_map/all_to_all | solution.py:95
  266.2 1.8 reshape.188
  268.0 2.7 slice.71
  270.7 2.6 copy.78
  273.3 2.1 select_bitcast_fusion.1
  275.4 2.0 pad_maximum_fusion
  277.3 4.7 %copy.77 = bf16[512,3072]{1,0:T(8,128)(2,1)} copy(bf16[512,3072]{0,1:T(8,128)(2,1)} %bitcast.195) | data formatting | bytes 6291456 | tf_op jit(solution)/shard_map/dot_general | solution.py:101
  282.0 3.4 convolution_bitcast_fusion.2
  285.4 1.3 fusion.24
  288.4 1.5 fusion.70
  290.5 1.8 copy.85
  292.3 3.3 convert_element_type.93
  295.5 2.3 copy.86
  299.9 3.1 convolution_convert_fusion.1
  303.6 3.1 copy.87
  306.7 63.8 %reduce-scatter.2.cloned.1.call-done = bf16[768,4,256]{2,0,1:T(8,128)(2,1)} async-done(((bf16[3072,4,256]{2,0,1:T(8,128)(2,1)}), bf16[768,4,256]{2,0,1:T(8,128)(2,1)}) %reduce-scatter.2.cloned.1.call-update) | async-done | bytes 1572880 | tf_op jit(solution)/shard_map/reduce_scatter | solution.py:120
  370.5 1.5 constant_dynamic-slice_fusion.3
  372.9 2.6 collective-permute-start.2
  375.5 4.0 collective-permute-start.3
  379.5 3.4 collective-permute-start.4
  382.9 11.2 %collective-permute-done.2 = bf16[192,4,256]{2,1,0:T(4,128)(2,1)S(1)} collective-permute-done((bf16[192,4,256]{2,1,0:T(4,128)(2,1)S(1)}, bf16[192,4,256]{2,1,0:T(4,128)(2,1)S(1)}, u32[]{:S(2)}, u32[]{:S(2)}) %collective-permute-start.2) | collective-permute-done | bytes 393248 | tf_op jit(solution)/shard_map/ppermute | solution.py:127
  394.1 12.5 %collective-permute-done.3 = bf16[192,4,256]{2,1,0:T(4,128)(2,1)S(1)} collective-permute-done((bf16[192,4,256]{2,1,0:T(4,128)(2,1)S(1)}, bf16[192,4,256]{2,1,0:T(4,128)(2,1)S(1)}, u32[]{:S(2)}, u32[]{:S(2)}) %collective-permute-start.3) | collective-permute-done | bytes 393248 | tf_op jit(solution)/shard_map/ppermute | solution.py:127
  406.6 7.7 %collective-permute-done.4 = bf16[192,4,256]{2,1,0:T(4,128)(2,1)S(1)} collective-permute-done((bf16[192,4,256]{2,1,0:T(4,128)(2,1)S(1)}, bf16[192,4,256]{2,1,0:T(4,128)(2,1)S(1)}, u32[]{:S(2)}, u32[]{:S(2)}) %collective-permute-start.4) | collective-permute-done | bytes 393248 | tf_op jit(solution)/shard_map/ppermute | solution.py:127
  414.3 1.4 fusion.31
  (58 shorter events, 13.2 us)
Async XLA Ops:
  6.5 157.1 %all-gather.2.cloned.1.call-start = ((), (), s32[]{:S(2)}) async-start(), calls=%async_computation.3 | async-start | bytes 13369344 | tf_op jit(solution)/shard_map/all_gather | solution.py:54
  174.4 1.7 copy-start.2
  194.5 2.2 copy-start.1
  196.7 3.8 collective-permute-start
  203.9 35.8 %all-to-all-start = ((bf16[8,192,512]{2,1,0:T(8,128)(2,1)}), bf16[8,192,512]{2,1,0:T(8,128)(2,1)}, u32[]{:S(2)}, u32[]{:S(2)}) async-start(bf16[8,192,512]{2,1,0:T(8,128)(2,1)} %fusion.7), calls=%async_computation | async-start | bytes 3145728 | tf_op jit(solution)/shard_map/all_to_all | solution.py:90
  220.1 150.4 %reduce-scatter.2.cloned.1.call-start = ((), (), s32[]{:S(2)}) async-start(), calls=%async_computation.4 | async-start | bytes 7864320 | tf_op jit(solution)/shard_map/reduce_scatter | solution.py:120
  266.2 7.1 %collective-permute-start.1 = (bf16[8,192,512]{2,1,0:T(8,128)(2,1)}, bf16[8,192,512]{2,1,0:T(8,128)(2,1)}, u32[]{:S(2)}, u32[]{:S(2)}) collective-permute-start(bf16[8,192,512]{2,1,0:T(8,128)(2,1)} %all_to_all.10), channel_id=1, source_target_pairs={{0,1},{1,0},{2,3},{3,2},{4,5},{5,4},{6,7},{7,6},{8,9},{9,8},{10,11... | collective-permute-start | bytes 4718600 | tf_op jit(solution)/shard_map/ppermute | solution.py:96
  290.4 7.4 %copy-start.4 = (bf16[512,256,1,1]{1,0,2,3:T(8,128)(2,1)S(1)}, bf16[512,256,1,1]{1,0,2,3:T(8,128)(2,1)}, u32[]{:S(2)}) copy-start(bf16[512,256,1,1]{1,0,2,3:T(8,128)(2,1)} %reshape.188) | copy-start | bytes 786436
  292.3 5.6 %copy-start = (bf16[8,2,192,512]{3,2,1,0:T(8,128)(2,1)S(1)}, bf16[8,2,192,512]{3,2,1,0:T(8,128)(2,1)}, u32[]{:S(2)}) copy-start(bf16[8,2,192,512]{3,2,1,0:T(8,128)(2,1)} %pad_maximum_fusion) | copy-start | bytes 9437188
  297.8 1.9 copy-start.3
  297.8 2.1 copy-start.5
  372.9 21.1 %collective-permute-start.2 = (bf16[192,4,256]{2,1,0:T(4,128)(2,1)S(1)}, bf16[192,4,256]{2,1,0:T(4,128)(2,1)S(1)}, u32[]{:S(2)}, u32[]{:S(2)}) collective-permute-start(bf16[192,4,256]{2,1,0:T(4,128)(2,1)S(1)} %bitcast.214), channel_id=1, source_target_pairs={{0,64},{64,128},{128,192},{192,0},{1,65},{65,129},{129,193},{193,1... | collective-permute-start | bytes 1179656 | tf_op jit(solution)/shard_map/ppermute | solution.py:127
  375.5 31.1 %collective-permute-start.3 = (bf16[192,4,256]{2,1,0:T(4,128)(2,1)S(1)}, bf16[192,4,256]{2,1,0:T(4,128)(2,1)S(1)}, u32[]{:S(2)}, u32[]{:S(2)}) collective-permute-start(bf16[192,4,256]{2,1,0:T(4,128)(2,1)S(1)} %bitcast.213), channel_id=1, source_target_pairs={{0,128},{64,192},{128,0},{192,64},{1,129},{65,193},{129,1},{193,65... | collective-permute-start | bytes 1179656 | tf_op jit(solution)/shard_map/ppermute | solution.py:127
  379.5 34.8 %collective-permute-start.4 = (bf16[192,4,256]{2,1,0:T(4,128)(2,1)S(1)}, bf16[192,4,256]{2,1,0:T(4,128)(2,1)S(1)}, u32[]{:S(2)}, u32[]{:S(2)}) collective-permute-start(bf16[192,4,256]{2,1,0:T(4,128)(2,1)S(1)} %bitcast.212), channel_id=1, source_target_pairs={{0,192},{64,0},{128,64},{192,128},{1,193},{65,1},{129,65},{193,129... | collective-permute-start | bytes 1179656 | tf_op jit(solution)/shard_map/ppermute | solution.py:127
Sparse Core Ops, SparseCore 0:
  12.2 151.3 all-gather.1
  306.8 63.6 reduce-scatter.1

commit v10 on v9

--- a/solution.py
+++ b/solution.py
@@ -121,7 +121,7 @@
     blocks = summed.reshape(n_hi, share_rows, 4, head_cols)
     hi_index = lax.axis_index("z_hi")
     total = lax.dynamic_index_in_dim(blocks, hi_index, 0, keepdims=False).astype(jnp.float32)
-    for shift in range(1, n_hi):
+    for shift in sorted(range(1, n_hi), key=lambda k: -min(k, n_hi - k)):
         outgoing = lax.dynamic_index_in_dim(blocks, (hi_index + shift) % n_hi, 0, keepdims=False)
         pairs = [(i, (i + shift) % n_hi) for i in range(n_hi)]
         total = total + lax.ppermute(outgoing, "z_hi", pairs).astype(jnp.float32)

time: 424 us -> 424 us (level)
  no operation moved by 1% of the time
where the time goes in v10:
time: 424 us; the launch traced here: 422 us
  waiting for transfers between devices  262 us (62%)
  local copies, waits for them, and re-layouts  44.5 us (10%)
  matrix products  32.8 us (8%)
  starting transfers between devices  26.1 us (6%)
  blocking collectives  24.5 us (6%)
  other arithmetic  18.5 us (4%)
  between operations  13.8 us (3%)
    all_gather x1, waiting for transfers between devices, body(): gathered = lax.all_gather(local.T, FSDP, axis=1, tiled=True)  144 us
    reduce_scatter x1, waiting for transfers between devices, body(): summed = lax.psum_scatter(summed, 'x', scatter_dimension=0, tiled=True)  63.8 us
    ppermute x3, waiting for transfers between devices, body(): total = total + lax.ppermute(outgoing, 'z_hi', pairs).astype(jnp.float32)  30.8 us
    all_to_all x1, blocking collectives, body(): on_chip = lax.all_to_all(spread, ('z_lo', 'y'), 0, 0)  24.5 us
    all_to_all x1, waiting for transfers between devices, body(): arrived = lax.all_to_all(pair_sum.astype(jnp.bfloat16), ('z_lo', 'y'), 0, 0)  18.9 us
    all_to_all x1, starting transfers between devices, body(): arrived = lax.all_to_all(pair_sum.astype(jnp.bfloat16), ('z_lo', 'y'), 0, 0)  16.2 us
    ppermute x3, starting transfers between devices, body(): total = total + lax.ppermute(outgoing, 'z_hi', pairs).astype(jnp.float32)  9.94 us
    dot_general x1, matrix products, cross_rows(): lax.dot_general(left, right, (((1,), (1,)), ((), ())), preferred_element_...  9.42 us
  transfers between devices with their start and end apart: 8, of which 7 were waited for; matrix products, arithmetic and copies ran while one was open for 4% of the time, Pallas kernels for 0%

profile of v10, /device:TPU:8, one launch (start us, length us, event | category | flops | bytes accessed | tf_op | source)
XLA Modules:
  0.0 422.0 jit_solution(7690654726230957890)
XLA Ops:
  6.5 1.2 slice.48
  7.8 1.2 slice.49
  9.0 2.0 pad_maximum_fusion.1
  11.0 1.1 copy.112
  12.1 3.2 copy.60
  16.7 2.5 fusion.5
  19.1 144.5 %all-gather.2.cloned.1.call-done = bf16[2048,3072]{0,1:T(8,128)(2,1)} async-done(((bf16[2048,192]{0,1:T(8,128)(2,1)}), bf16[2048,3072]{0,1:T(8,128)(2,1)}) %all-gather.2.cloned.1.call-update) | async-done | bytes 12582928 | tf_op jit(solution)/shard_map/all_gather | solution.py:54
  163.6 9.4 %fusion.10 = bf16[512,1536]{1,0:T(8,128)(2,1)S(1)} fusion(bf16[512,3072]{0,1:T(8,128)(2,1)} %fusion.5, bf16[2048,3072]{0,1:T(8,128)(2,1)} %all-gather.2.cloned.1.call-done), kind=kOutput, calls=%fused_computation.17 | convolution fusion | flops 4832624640 | bytes 14155776 | tf_op jit(solution)/shard_map/dot_general | solution.py:34
  174.6 1.2 copy.62
  176.6 1.2 fusion.76
  177.8 1.5 fusion.55
  179.3 1.3 fusion.23
  180.6 1.1 fusion.40
  181.7 1.3 fusion.77
  183.0 1.4 fusion.25
  184.4 1.8 copy.73
  186.2 1.7 copy.127
  187.9 1.8 copy.75
  190.7 3.7 convolution_convert_fusion
  194.5 1.4 dynamic-slice_bitcast_fusion
  196.7 3.7 collective-permute-done
  200.4 3.5 fusion.7
  203.9 16.2 %all-to-all-start = ((bf16[8,192,512]{2,1,0:T(8,128)(2,1)}), bf16[8,192,512]{2,1,0:T(8,128)(2,1)}, u32[]{:S(2)}, u32[]{:S(2)}) async-start(bf16[8,192,512]{2,1,0:T(8,128)(2,1)} %fusion.7), calls=%async_computation | async-start | bytes 3145728 | tf_op jit(solution)/shard_map/all_to_all | solution.py:90
  220.9 18.9 %all-to-all-done = bf16[8,192,512]{2,1,0:T(8,128)(2,1)} async-done(((bf16[8,192,512]{2,1,0:T(8,128)(2,1)}), bf16[8,192,512]{2,1,0:T(8,128)(2,1)}, u32[]{:S(2)}, u32[]{:S(2)}) %all-to-all-start) | async-done | bytes 1572896 | tf_op jit(solution)/shard_map/all_to_all | solution.py:90
  239.8 1.7 convert_reduce_fusion.1
  241.7 24.5 %all_to_all.10 = bf16[8,192,512]{2,1,0:T(8,128)(2,1)} all-to-all(bf16[8,192,512]{2,1,0:T(8,128)(2,1)S(1)} %broadcast_in_dim.12), channel_id=1, replica_groups=mesh['z_hi'=4,'x'=4,'z_lo'=2,'y'=4,'core'=2] {'z_lo','y'}, dimensions={0} | all-to-all | bytes 3145728 | tf_op jit(solution)/shard_map/all_to_all | solution.py:95
  266.2 1.8 reshape.188
  268.0 2.7 slice.71
  270.7 2.6 copy.78
  273.3 2.1 select_bitcast_fusion.1
  275.4 2.0 pad_maximum_fusion
  277.3 4.7 %copy.77 = bf16[512,3072]{1,0:T(8,128)(2,1)} copy(bf16[512,3072]{0,1:T(8,128)(2,1)} %bitcast.195) | data formatting | bytes 6291456 | tf_op jit(solution)/shard_map/dot_general | solution.py:101
  282.0 3.4 convolution_bitcast_fusion.2
  285.4 1.3 fusion.24
  288.4 1.5 fusion.70
  290.5 1.8 copy.85
  292.3 3.3 convert_element_type.93
  295.5 2.3 copy.86
  299.9 3.1 convolution_convert_fusion.1
  303.6 3.1 copy.87
  306.7 63.8 %reduce-scatter.2.cloned.1.call-done = bf16[768,4,256]{2,0,1:T(8,128)(2,1)} async-done(((bf16[3072,4,256]{2,0,1:T(8,128)(2,1)}), bf16[768,4,256]{2,0,1:T(8,128)(2,1)}) %reduce-scatter.2.cloned.1.call-update) | async-done | bytes 1572880 | tf_op jit(solution)/shard_map/reduce_scatter | solution.py:120
  370.5 1.5 constant_dynamic-slice_fusion.3
  372.9 5.8 %collective-permute-start.2 = (bf16[192,4,256]{2,1,0:T(4,128)(2,1)S(1)}, bf16[192,4,256]{2,1,0:T(4,128)(2,1)S(1)}, u32[]{:S(2)}, u32[]{:S(2)}) collective-permute-start(bf16[192,4,256]{2,1,0:T(4,128)(2,1)S(1)} %bitcast.214), channel_id=1, source_target_pairs={{0,128},{64,192},{128,0},{192,64},{1,129},{65,193},{129,1},{193,65... | collective-permute-start | bytes 1179656 | tf_op jit(solution)/shard_map/ppermute | solution.py:127
  379.5 3.4 collective-permute-start.4
  382.9 15.3 %collective-permute-done.2 = bf16[192,4,256]{2,1,0:T(4,128)(2,1)S(1)} collective-permute-done((bf16[192,4,256]{2,1,0:T(4,128)(2,1)S(1)}, bf16[192,4,256]{2,1,0:T(4,128)(2,1)S(1)}, u32[]{:S(2)}, u32[]{:S(2)}) %collective-permute-start.2) | collective-permute-done | bytes 393248 | tf_op jit(solution)/shard_map/ppermute | solution.py:127
  398.2 8.9 %collective-permute-done.3 = bf16[192,4,256]{2,1,0:T(4,128)(2,1)S(1)} collective-permute-done((bf16[192,4,256]{2,1,0:T(4,128)(2,1)S(1)}, bf16[192,4,256]{2,1,0:T(4,128)(2,1)S(1)}, u32[]{:S(2)}, u32[]{:S(2)}) %collective-permute-start.3) | collective-permute-done | bytes 393248 | tf_op jit(solution)/shard_map/ppermute | solution.py:127
  407.1 6.6 %collective-permute-done.4 = bf16[192,4,256]{2,1,0:T(4,128)(2,1)S(1)} collective-permute-done((bf16[192,4,256]{2,1,0:T(4,128)(2,1)S(1)}, bf16[192,4,256]{2,1,0:T(4,128)(2,1)S(1)}, u32[]{:S(2)}, u32[]{:S(2)}) %collective-permute-start.4) | collective-permute-done | bytes 393248 | tf_op jit(solution)/shard_map/ppermute | solution.py:127
  413.7 1.4 fusion.31
  (58 shorter events, 12.9 us)
Async XLA Ops:
  6.5 157.1 %all-gather.2.cloned.1.call-start = ((), (), s32[]{:S(2)}) async-start(), calls=%async_computation.3 | async-start | bytes 13369344 | tf_op jit(solution)/shard_map/all_gather | solution.py:54
  174.4 1.7 copy-start.2
  194.5 2.2 copy-start.1
  196.7 3.8 collective-permute-start
  203.9 35.8 %all-to-all-start = ((bf16[8,192,512]{2,1,0:T(8,128)(2,1)}), bf16[8,192,512]{2,1,0:T(8,128)(2,1)}, u32[]{:S(2)}, u32[]{:S(2)}) async-start(bf16[8,192,512]{2,1,0:T(8,128)(2,1)} %fusion.7), calls=%async_computation | async-start | bytes 3145728 | tf_op jit(solution)/shard_map/all_to_all | solution.py:90
  220.1 150.4 %reduce-scatter.2.cloned.1.call-start = ((), (), s32[]{:S(2)}) async-start(), calls=%async_computation.4 | async-start | bytes 7864320 | tf_op jit(solution)/shard_map/reduce_scatter | solution.py:120
  266.2 7.1 %collective-permute-start.1 = (bf16[8,192,512]{2,1,0:T(8,128)(2,1)}, bf16[8,192,512]{2,1,0:T(8,128)(2,1)}, u32[]{:S(2)}, u32[]{:S(2)}) collective-permute-start(bf16[8,192,512]{2,1,0:T(8,128)(2,1)} %all_to_all.10), channel_id=1, source_target_pairs={{0,1},{1,0},{2,3},{3,2},{4,5},{5,4},{6,7},{7,6},{8,9},{9,8},{10,11... | collective-permute-start | bytes 4718600 | tf_op jit(solution)/shard_map/ppermute | solution.py:96
  290.4 7.4 %copy-start.4 = (bf16[512,256,1,1]{1,0,2,3:T(8,128)(2,1)S(1)}, bf16[512,256,1,1]{1,0,2,3:T(8,128)(2,1)}, u32[]{:S(2)}) copy-start(bf16[512,256,1,1]{1,0,2,3:T(8,128)(2,1)} %reshape.188) | copy-start | bytes 786436
  292.3 5.6 %copy-start = (bf16[8,2,192,512]{3,2,1,0:T(8,128)(2,1)S(1)}, bf16[8,2,192,512]{3,2,1,0:T(8,128)(2,1)}, u32[]{:S(2)}) copy-start(bf16[8,2,192,512]{3,2,1,0:T(8,128)(2,1)} %pad_maximum_fusion) | copy-start | bytes 9437188
  297.8 1.9 copy-start.3
  297.8 2.1 copy-start.5
  372.9 25.2 %collective-permute-start.2 = (bf16[192,4,256]{2,1,0:T(4,128)(2,1)S(1)}, bf16[192,4,256]{2,1,0:T(4,128)(2,1)S(1)}, u32[]{:S(2)}, u32[]{:S(2)}) collective-permute-start(bf16[192,4,256]{2,1,0:T(4,128)(2,1)S(1)} %bitcast.214), channel_id=1, source_target_pairs={{0,128},{64,192},{128,0},{192,64},{1,129},{65,193},{129,1},{193,65... | collective-permute-start | bytes 1179656 | tf_op jit(solution)/shard_map/ppermute | solution.py:127
  378.8 28.3 %collective-permute-start.3 = (bf16[192,4,256]{2,1,0:T(4,128)(2,1)S(1)}, bf16[192,4,256]{2,1,0:T(4,128)(2,1)S(1)}, u32[]{:S(2)}, u32[]{:S(2)}) collective-permute-start(bf16[192,4,256]{2,1,0:T(4,128)(2,1)S(1)} %bitcast.213), channel_id=1, source_target_pairs={{0,64},{64,128},{128,192},{192,0},{1,65},{65,129},{129,193},{193,1... | collective-permute-start | bytes 1179656 | tf_op jit(solution)/shard_map/ppermute | solution.py:127
  379.5 34.2 %collective-permute-start.4 = (bf16[192,4,256]{2,1,0:T(4,128)(2,1)S(1)}, bf16[192,4,256]{2,1,0:T(4,128)(2,1)S(1)}, u32[]{:S(2)}, u32[]{:S(2)}) collective-permute-start(bf16[192,4,256]{2,1,0:T(4,128)(2,1)S(1)} %bitcast.212), channel_id=1, source_target_pairs={{0,192},{64,0},{128,64},{192,128},{1,193},{65,1},{129,65},{193,129... | collective-permute-start | bytes 1179656 | tf_op jit(solution)/shard_map/ppermute | solution.py:127
Sparse Core Ops, SparseCore 0:
  12.2 151.3 all-gather.1
  306.8 63.6 reduce-scatter.1
